TPU v7x, 32 devices: a whole 2x2x4 slice. The times are simulated.
32 devices in a mesh: dom: 16 (over z, y, x), task: 2 (over core).
Axes of the slice: x: 2, y: 2, z: 4, core: 2. Of those that a mesh axis runs over, the one named last changes fastest.
Arguments:
- positions: float32 [1024, 3, 128], P('dom'), may hold values from 0 to 1
- velocities: float32 [1024, 3, 128], P('dom'), may hold values from -5 to 5
- masses: float32 [1024, 128], P('dom'), may hold values from 0.005 to 0.02
- smoothing: float32 [1024, 128], P('dom'), may hold values from 0.35 to 0.7
- energy: float32 [1024, 128], P('dom'), may hold values from 0.5 to 2
- block_counts: int32 [1024], P('dom'), may hold values from 32 to 128, as said below
- send_lists: int32 [16, 8, 24], P('dom'), may hold values from 0 to 63, as said below
- task_lists: int32 [16, 2, 128], P('dom', 'task'), may hold values from 0 to 16383, as said below
- task_counts: int32 [16, 2], P('dom', 'task'), may hold values from 8 to 128, as said below
Outputs:
- density: float32 [1024, 128], P('dom')
- acceleration: float32 [1024, 3, 128], P('dom')
- energy_rate: float32 [1024, 128], P('dom')
Inputs may be any that keep to these rules, and one draw needn't show every extreme that they name: `block_counts`: the valid particles of a block are its first ones; every domain has a full block. `send_lists`: the 24 entries of one domain's list for one direction are different blocks of that domain. `task_lists`: the tasks of a domain (the first task_counts entries of each of its two lists) are all different pairs; entries beyond a list's count are not tasks. `task_counts`: in each domain one of the two devices holds 96 to 128 tasks and the other 8 to 16; which one is drawn.
All inputs are finite; a program needn't handle non-finite values.
Results may differ from a plain program's by a relative error of at most 0.0003.
Values sent between devices are 32-bit elements; how exact they have to be, the bound alone decides.
No kernel may reach another device: no remote copies, remote signals or barrier semaphores. Data moves between devices by JAX's collectives and lax.ppermute only.
A program may use at most 64 MiB of HBM per device.

v0:
```python
import math

import jax
import jax.numpy as jnp
import numpy as np
from jax import lax
from jax.sharding import PartitionSpec as P

GY = 8


GAMMA = 5.0 / 3.0
VISC_ALPHA = 0.8
KERNEL_NORM = 8.0 / math.pi
DIRECTIONS = ((-1, -1), (-1, 0), (-1, 1), (0, -1), (0, 1), (1, -1), (1, 0), (1, 1))


def passed_along(block, axis, distance):
    devices = range(lax.axis_size(axis))
    route = [((i - distance) % len(devices), i) for i in devices]
    return lax.ppermute(block, axis, route)


def spline_value(ratio):
    inner = 1.0 - 6.0 * ratio * ratio + 6.0 * ratio * ratio * ratio
    outer = 2.0 * jnp.maximum(1.0 - ratio, 0.0) ** 3
    return jnp.where(ratio < 0.5, inner, outer)


def spline_slope(ratio):
    inner = -12.0 + 18.0 * ratio
    outer = -6.0 * jnp.maximum(1.0 - ratio, 0.0) ** 2 / jnp.maximum(ratio, 0.5)
    return jnp.where(ratio < 0.5, inner, outer)


def active_flags(source_particle_count, self_block_pair, block_width):
    column = jnp.arange(block_width, dtype=jnp.int32)
    present = column[None, :] < source_particle_count
    distinct = jnp.logical_or(column[:, None] != column[None, :], jnp.logical_not(self_block_pair))
    return jnp.logical_and(present, distinct).astype(jnp.float32)


def geometry(target_feat, source_feat):
    separation = target_feat[0:3, :, None] - source_feat[0:3, None, :]
    dist_sq = jnp.sum(separation * separation, axis=0)
    return (separation, dist_sq, jnp.sqrt(dist_sq))


def pair_density(target_feat, source_feat, active_slot):
    separation, dist_sq, radius = geometry(target_feat, source_feat)
    h_target = target_feat[7][:, None]
    kernel = KERNEL_NORM / h_target**3 * spline_value(radius / h_target)
    return jnp.sum(source_feat[6][None, :] * active_slot * kernel, axis=1)


def pair_force(target_feat, source_feat, active_slot, rho_target, rho_source):
    separation, dist_sq, radius = geometry(target_feat, source_feat)
    h_target = target_feat[7][:, None]
    h_source = source_feat[7][None, :]
    press_target = ((GAMMA - 1.0) * target_feat[8] / rho_target)[:, None]
    press_source = ((GAMMA - 1.0) * source_feat[8] / rho_source)[None, :]
    sound_target = jnp.sqrt(GAMMA * (GAMMA - 1.0) * target_feat[8])[:, None]
    sound_source = jnp.sqrt(GAMMA * (GAMMA - 1.0) * source_feat[8])[None, :]
    slope_target = KERNEL_NORM / h_target**5 * spline_slope(radius / h_target)
    slope_source = KERNEL_NORM / h_source**5 * spline_slope(radius / h_source)
    approach = jnp.sum((target_feat[3:6, :, None] - source_feat[3:6, None, :]) * separation, axis=0)
    h_mean = 0.5 * (h_target + h_source)
    visc_mu = h_mean * jnp.minimum(approach, 0.0) / (dist_sq + 0.01 * h_mean * h_mean)
    rho_mean = 0.5 * (rho_target[:, None] + rho_source[None, :])
    viscosity = (
        -VISC_ALPHA * 0.5 * (sound_target + sound_source) * visc_mu
        + 2.0 * VISC_ALPHA * visc_mu * visc_mu
    ) / rho_mean
    weight = source_feat[6][None, :] * active_slot
    slope_mean = 0.5 * (slope_target + slope_source)
    pull = weight * (
        press_target * slope_target + press_source * slope_source + viscosity * slope_mean
    )
    accel = -jnp.sum(pull[None] * separation, axis=2)
    heating = jnp.sum(
        weight * (press_target * slope_target + 0.5 * viscosity * slope_mean) * approach, axis=1
    )
    return jnp.concatenate([accel, heating[None]], axis=0)


def pick_rows(table, row_ids):
    equal = row_ids[:, None] == jnp.arange(table.shape[0], dtype=jnp.int32)[None, :]
    if table.dtype == jnp.int32:
        return jnp.sum(jnp.where(equal, table[None, :], 0), axis=1).astype(jnp.int32)
    flat = table.reshape(table.shape[0], -1)
    picked = jnp.dot(equal.astype(jnp.float32), flat, precision=lax.Precision.HIGHEST)
    return picked.reshape(row_ids.shape + table.shape[1:])


def fetch_ghosts(own_parts, send_rows):
    arrived = {}
    for number, (col_step, row_step) in enumerate(DIRECTIONS):
        row_ids = send_rows[number]
        arrived[col_step, row_step] = passed_along(
            tuple((pick_rows(member, row_ids) for member in own_parts)),
            "dom",
            col_step * GY + row_step,
        )
    return tuple(
        (
            jnp.concatenate([arrived[heading][member_index] for heading in DIRECTIONS], axis=0)
            for member_index in range(len(own_parts))
        )
    )


def place_ghosts(ghost_feat, per_direction):
    offsets = np.repeat(np.array(DIRECTIONS, dtype=np.float32), per_direction, axis=0)
    shifted = ghost_feat[:, 0:2, :] - jnp.asarray(offsets, dtype=ghost_feat.dtype)[:, :, None]
    return jnp.concatenate([shifted, ghost_feat[:, 2:, :]], axis=1)


def pick_tasks(task_lists, task_counts):
    both_lists, both_counts = (
        lax.all_gather(task_lists, "task", axis=1, tiled=True),
        lax.all_gather(task_counts, "task", axis=1, tiled=True),
    )
    list_pair = both_lists[0]
    count_pair = both_counts[0]
    capacity = list_pair.shape[1]
    overall = count_pair[0] + count_pair[1]
    member_rank = lax.axis_index("task")
    my_count = (overall + 1 - member_rank) // 2
    places = 2 * jnp.arange(capacity, dtype=jnp.int32) + member_rank
    first_pick = list_pair[0][jnp.clip(places, 0, capacity - 1)]
    second_pick = list_pair[1][jnp.clip(places - count_pair[0], 0, capacity - 1)]
    my_list = jnp.where(places < count_pair[0], first_pick, second_pick)
    return (my_list, my_count)


def run_tasks(task_row, task_total, tables, counts_table, own_count, task_fn, start_value):
    per_turn = 4
    source_total = counts_table.shape[0]
    batches = task_row.reshape(-1, per_turn)
    block_ids = jnp.arange(own_count, dtype=jnp.int32)

    def one_turn(step_index, running):
        values = batches[step_index]
        slot_ids = step_index * per_turn + jnp.arange(per_turn, dtype=jnp.int32)
        living = (slot_ids < task_total).astype(jnp.float32)
        targets = values // source_total
        sources = values % source_total
        target_rows = tuple((pick_rows(table, targets) for table in tables))
        source_rows = tuple((pick_rows(table, sources) for table in tables))
        source_counts = pick_rows(counts_table, sources)
        pieces = jax.vmap(task_fn)(target_rows, source_rows, source_counts, targets == sources)
        selector = (block_ids[:, None] == targets[None, :]).astype(jnp.float32) * living[None, :]
        return running + jnp.tensordot(selector, pieces, axes=1, precision=lax.Precision.HIGHEST)

    rounds = (task_total + per_turn - 1) // per_turn
    return lax.fori_loop(0, rounds, one_turn, start_value)


def local(
    positions,
    velocities,
    masses,
    smoothing,
    energy,
    block_counts,
    send_lists,
    task_lists,
    task_counts,
):
    own_feat = jnp.concatenate(
        [positions, velocities, masses[:, None], smoothing[:, None], energy[:, None]], axis=1
    )
    own_count = own_feat.shape[0]
    block_width = own_feat.shape[2]
    send_rows = send_lists[0]
    ghost_feat, ghost_counts = fetch_ghosts((own_feat, block_counts), send_rows)
    ghost_feat = place_ghosts(ghost_feat, send_rows.shape[1])
    all_feat = jnp.concatenate([own_feat, ghost_feat], axis=0)
    every_block_counts = jnp.concatenate([block_counts, ghost_counts], axis=0)
    my_list, my_count = pick_tasks(task_lists, task_counts)

    def density_task(target_rows, source_rows, source_count, same_block):
        active_slot = active_flags(source_count, same_block, block_width)
        return pair_density(target_rows[0], source_rows[0], active_slot)

    partial_rho = run_tasks(
        my_list,
        my_count,
        (all_feat,),
        every_block_counts,
        own_count,
        density_task,
        jnp.zeros((own_count, block_width), jnp.float32),
    )
    rho_own = lax.psum(partial_rho, "task") + masses * KERNEL_NORM / smoothing**3
    (ghost_rho,) = fetch_ghosts((rho_own,), send_rows)
    all_rho = jnp.concatenate([rho_own, ghost_rho], axis=0)

    def force_task(target_rows, source_rows, source_count, same_block):
        active_slot = active_flags(source_count, same_block, block_width)
        return pair_force(
            target_rows[0], source_rows[0], active_slot, target_rows[1], source_rows[1]
        )

    partial_force = run_tasks(
        my_list,
        my_count,
        (all_feat, all_rho),
        every_block_counts,
        own_count,
        force_task,
        jnp.zeros((own_count, 4, block_width), jnp.float32),
    )
    forces = lax.psum(partial_force, "task")
    valid = jnp.arange(block_width, dtype=jnp.int32)[None, :] < block_counts[:, None]
    density = jnp.where(valid, rho_own, 0.0)
    acceleration = jnp.where(valid[:, None, :], forces[:, 0:3], 0.0)
    energy_rate = jnp.where(valid, forces[:, 3], 0.0)
    return (density, acceleration, energy_rate)


def solution(mesh):
    placed = (
        P("dom", None, None),
        P("dom", None, None),
        P("dom", None),
        P("dom", None),
        P("dom", None),
        P("dom"),
        P("dom", None, None),
        P("dom", "task", None),
        P("dom", "task"),
    )
    return jax.shard_map(
        local,
        mesh=mesh,
        in_specs=placed,
        out_specs=(P("dom", None), P("dom", None, None), P("dom", None)),
        check_vma=False,
    )
```

profile of v0, /device:TPU:0, one launch (start us, length us, event | category | flops | bytes accessed | tf_op | source)
XLA Modules:
  0.0 248.0 jit_solution(15560370723070966730)
XLA Ops:
  12.5 5.0 %collective-permute-start.8 = (f32[24,9,128]{2,0,1:T(8,128)S(1)}, f32[24,9,128]{2,0,1:T(8,128)S(1)}, u32[]{:S(2)}, u32[]{:S(2)}) collective-permute-start(f32[24,9,128]{2,0,1:T(8,128)S(1)} %fusion.77), channel_id=1, source_target_pairs={{18,0},{20,2},{22,4},{24,6},{26,8},{28,10},{30,12},{0,14},{2,16},{... | collective-permute-start | bytes 331784 | tf_op jit(solution)/shard_map/ppermute | solution.py:21
  17.8 2.7 %collective-permute-start.9 = (f32[24,9,128]{2,0,1:T(8,128)S(1)}, f32[24,9,128]{2,0,1:T(8,128)S(1)}, u32[]{:S(2)}, u32[]{:S(2)}) collective-permute-start(f32[24,9,128]{2,0,1:T(8,128)S(1)} %fusion.75), channel_id=1, source_target_pairs={{16,0},{18,2},{20,4},{22,6},{24,8},{26,10},{28,12},{30,14},{0,16},... | collective-permute-start | bytes 331784 | tf_op jit(solution)/shard_map/ppermute | solution.py:21
  21.4 3.5 %collective-permute-start = (s32[24]{0:T(128)S(1)}, s32[24]{0:T(128)S(1)}, u32[]{:S(2)}, u32[]{:S(2)}) collective-permute-start(s32[24]{0:T(128)S(1)} %get-tuple-element.337), channel_id=1, source_target_pairs={{18,0},{20,2},{22,4},{24,6},{26,8},{28,10},{30,12},{0,14},{2,16},{... | collective-permute-start | bytes 296 | tf_op jit(solution)/shard_map/ppermute | solution.py:21
  28.5 1.8 all-reduce
  31.6 1.8 all_gather.7
  33.5 1.2 gather_fusion
  34.8 1.2 gather_fusion.1
  38.2 1.1 collective-permute-start.2
  39.2 4.8 %collective-permute-start.3 = (s32[24]{0:T(128)S(1)}, s32[24]{0:T(128)S(1)}, u32[]{:S(2)}, u32[]{:S(2)}) collective-permute-start(s32[24]{0:T(128)S(1)} %get-tuple-element.333), channel_id=1, source_target_pairs={{2,0},{4,2},{6,4},{8,6},{10,8},{12,10},{14,12},{16,14},{18,16},{20... | collective-permute-start | bytes 296 | tf_op jit(solution)/shard_map/ppermute | solution.py:21
  44.2 1.2 collective-permute-done.3
  45.4 3.2 %collective-permute-start.5 = (s32[24]{0:T(128)S(1)}, s32[24]{0:T(128)S(1)}, u32[]{:S(2)}, u32[]{:S(2)}) collective-permute-start(s32[24]{0:T(128)S(1)} %get-tuple-element.335), channel_id=1, source_target_pairs={{18,0},{20,2},{22,4},{24,6},{26,8},{28,10},{30,12},{0,14},{2,16},{... | collective-permute-start | bytes 296 | tf_op jit(solution)/shard_map/ppermute | solution.py:21
  48.5 2.7 %collective-permute-done.4 = s32[24]{0:T(128)S(1)} collective-permute-done((s32[24]{0:T(128)S(1)}, s32[24]{0:T(128)S(1)}, u32[]{:S(2)}, u32[]{:S(2)}) %collective-permute-start.4) | collective-permute-done | bytes 128 | tf_op jit(solution)/shard_map/ppermute | solution.py:21
  51.8 2.8 %collective-permute-start.7 = (s32[24]{0:T(128)S(1)}, s32[24]{0:T(128)S(1)}, u32[]{:S(2)}, u32[]{:S(2)}) collective-permute-start(s32[24]{0:T(128)S(1)} %get-tuple-element.330), channel_id=1, source_target_pairs={{14,0},{16,2},{18,4},{20,6},{22,8},{24,10},{26,12},{28,14},{30,16}... | collective-permute-start | bytes 296 | tf_op jit(solution)/shard_map/ppermute | solution.py:21
  54.6 1.1 collective-permute-done.6
  55.7 1.7 collective-permute-start.11
  57.4 2.6 %collective-permute-start.12 = (f32[24,9,128]{2,0,1:T(8,128)S(1)}, f32[24,9,128]{2,0,1:T(8,128)S(1)}, u32[]{:S(2)}, u32[]{:S(2)}) collective-permute-start(f32[24,9,128]{2,0,1:T(8,128)S(1)} %fusion.69), channel_id=1, source_target_pairs={{30,0},{0,2},{2,4},{4,6},{6,8},{8,10},{10,12},{12,14},{14,16},{16,... | collective-permute-start | bytes 331784 | tf_op jit(solution)/shard_map/ppermute | solution.py:21
  60.1 2.0 collective-permute-start.13
  62.1 1.8 collective-permute-start.14
  64.7 2.2 collective-permute-done.12
  67.0 5.3 %collective-permute-done.13 = f32[24,9,128]{2,0,1:T(8,128)S(1)} collective-permute-done((f32[24,9,128]{2,0,1:T(8,128)S(1)}, f32[24,9,128]{2,0,1:T(8,128)S(1)}, u32[]{:S(2)}, u32[]{:S(2)}) %collective-permute-start.13) | collective-permute-done | bytes 110624 | tf_op jit(solution)/shard_map/ppermute | solution.py:21
  72.5 1.2 collective-permute-done.15
  74.4 46.5 %while.26 = (s32[]{:T(128)}, f32[64,128]{1,0:T(8,128)S(1)}, s32[]{:T(128)}, s32[32,4]{1,0:T(8,128)S(1)}, s32[]{:T(128)}, /*index=5*/s32[256]{0:T(256)S(1)}, f32[...) while((s32[]{:T(128)}, f32[64,128]{1,0:T(8,128)S(1)}, ...), condition=%wide.region_12.13_spmd.clone, body=%wide.region_8.12_spmd.clone.sunk | while | flops 30506140 | bytes 3105155 | solution.py:156
  121.0 3.4 %psum.14 = f32[64,128]{1,0:T(8,128)S(1)} all-reduce(f32[64,128]{1,0:T(8,128)S(1)} %get-tuple-element.230), channel_id=1, replica_groups=mesh['dom'=16,'task'=2] {'task'}, use_global_device_ids=true, to_apply=%region_13.14 | all-reduce | flops 8192 | bytes 65536 | tf_op jit(solution)/shard_map/psum | solution.py:195
  126.2 4.0 %collective-permute-start.18 = (f32[24,128]{1,0:T(8,128)S(1)}, f32[24,128]{1,0:T(8,128)S(1)}, u32[]{:S(2)}, u32[]{:S(2)}) collective-permute-start(f32[24,128]{1,0:T(8,128)S(1)} %fusion.102), channel_id=1, source_target_pairs={{14,0},{16,2},{18,4},{20,6},{22,8},{24,10},{26,12},{28,14},{30,16}... | collective-permute-start | bytes 36872 | tf_op jit(solution)/shard_map/ppermute | solution.py:21
  130.2 2.2 collective-permute-start.19
  132.6 2.7 %collective-permute-start.21 = (f32[24,128]{1,0:T(8,128)S(1)}, f32[24,128]{1,0:T(8,128)S(1)}, u32[]{:S(2)}, u32[]{:S(2)}) collective-permute-start(f32[24,128]{1,0:T(8,128)S(1)} %fusion.96), channel_id=1, source_target_pairs={{18,0},{20,2},{22,4},{24,6},{26,8},{28,10},{30,12},{0,14},{2,16},{... | collective-permute-start | bytes 36872 | tf_op jit(solution)/shard_map/ppermute | solution.py:21
  135.3 3.3 %collective-permute-start.22 = (f32[24,128]{1,0:T(8,128)S(1)}, f32[24,128]{1,0:T(8,128)S(1)}, u32[]{:S(2)}, u32[]{:S(2)}) collective-permute-start(f32[24,128]{1,0:T(8,128)S(1)} %fusion.94), channel_id=1, source_target_pairs={{16,0},{18,2},{20,4},{22,6},{24,8},{26,10},{28,12},{30,14},{0,16},... | collective-permute-start | bytes 36872 | tf_op jit(solution)/shard_map/ppermute | solution.py:21
  140.3 3.7 %collective-permute-done.23 = f32[24,128]{1,0:T(8,128)S(1)} collective-permute-done((f32[24,128]{1,0:T(8,128)S(1)}, f32[24,128]{1,0:T(8,128)S(1)}, u32[]{:S(2)}, u32[]{:S(2)}) %collective-permute-start.23) | collective-permute-done | bytes 12320 | tf_op jit(solution)/shard_map/ppermute | solution.py:21
  144.1 79.1 %while.27 = (s32[]{:T(128)}, f32[64,4,128]{2,0,1:T(8,128)S(1)}, s32[]{:T(128)}, s32[32,4]{1,0:T(8,128)S(1)}, s32[]{:T(128)}, /*index=5*/s32[256]{0:T(256)S(1)}, ...) while((s32[]{:T(128)}, f32[64,4,128]{2,0,1:T(8,128)S(1)}, ...), condition=%wide.region_20.21_spmd.clone, body=%wide.region_14.20_spmd.clone.sunk | while | flops 38470300 | bytes 4753835 | solution.py:156
  223.9 14.2 %all-reduce.3.cloned.1.call-done = f32[64,4,128]{2,0,1:T(8,128)} async-done(((f32[64,4,128]{2,0,1:T(8,128)}), f32[64,4,128]{2,0,1:T(8,128)}) %all-reduce.3.cloned.1.call-update) | async-done | bytes 131088 | tf_op jit(solution)/shard_map/psum | solution.py:214
  238.1 1.5 fusion.89
  239.6 1.5 slice_select_fusion
  (803 shorter events, 140.9 us)
Async XLA Ops:
  7.2 14.0 %copy-start.3 = (s32[64]{0:T(128)S(1)}, s32[64]{0:T(128)}, u32[]{:S(2)}) copy-start(s32[64]{0:T(128)} %param.19) | copy-start | bytes 772
  7.2 231.0 %all-reduce.3.cloned.1.call-start = ((), (), s32[]{:S(2)}) async-start(), calls=%async_computation | async-start | bytes 262144 | tf_op jit(solution)/shard_map/psum | solution.py:214
  12.5 47.5 %collective-permute-start.8 = (f32[24,9,128]{2,0,1:T(8,128)S(1)}, f32[24,9,128]{2,0,1:T(8,128)S(1)}, u32[]{:S(2)}, u32[]{:S(2)}) collective-permute-start(f32[24,9,128]{2,0,1:T(8,128)S(1)} %fusion.77), channel_id=1, source_target_pairs={{18,0},{20,2},{22,4},{24,6},{26,8},{28,10},{30,12},{0,14},{2,16},{... | collective-permute-start | bytes 331784 | tf_op jit(solution)/shard_map/ppermute | solution.py:21
  17.5 9.5 %copy-start.6 = (u32[32]{0:T(128)S(1)}, u32[32]{0:T(128)}, u32[]{:S(2)}) copy-start(u32[32]{0:T(128)} %constant.273) | copy-start | bytes 388
  17.8 44.2 %collective-permute-start.9 = (f32[24,9,128]{2,0,1:T(8,128)S(1)}, f32[24,9,128]{2,0,1:T(8,128)S(1)}, u32[]{:S(2)}, u32[]{:S(2)}) collective-permute-start(f32[24,9,128]{2,0,1:T(8,128)S(1)} %fusion.75), channel_id=1, source_target_pairs={{16,0},{18,2},{20,4},{22,6},{24,8},{26,10},{28,12},{30,14},{0,16},... | collective-permute-start | bytes 331784 | tf_op jit(solution)/shard_map/ppermute | solution.py:21
  20.5 11.2 %copy-start.5 = (s32[1,1,128]{2,1,0:T(1,128)S(1)}, s32[1,1,128]{2,1,0:T(1,128)}, u32[]{:S(2)}) copy-start(s32[1,1,128]{2,1,0:T(1,128)} %param.21) | copy-start | bytes 1540
  20.7 43.1 %collective-permute-start.10 = (f32[24,9,128]{2,0,1:T(8,128)S(1)}, f32[24,9,128]{2,0,1:T(8,128)S(1)}, u32[]{:S(2)}, u32[]{:S(2)}) collective-permute-start(f32[24,9,128]{2,0,1:T(8,128)S(1)} %fusion.73), channel_id=1, source_target_pairs={{14,0},{16,2},{18,4},{20,6},{22,8},{24,10},{26,12},{28,14},{30,16}... | collective-permute-start | bytes 331784 | tf_op jit(solution)/shard_map/ppermute | solution.py:21
  21.4 16.7 %collective-permute-start = (s32[24]{0:T(128)S(1)}, s32[24]{0:T(128)S(1)}, u32[]{:S(2)}, u32[]{:S(2)}) collective-permute-start(s32[24]{0:T(128)S(1)} %get-tuple-element.337), channel_id=1, source_target_pairs={{18,0},{20,2},{22,4},{24,6},{26,8},{28,10},{30,12},{0,14},{2,16},{... | collective-permute-start | bytes 296 | tf_op jit(solution)/shard_map/ppermute | solution.py:21
  25.0 14.3 %collective-permute-start.1 = (s32[24]{0:T(128)S(1)}, s32[24]{0:T(128)S(1)}, u32[]{:S(2)}, u32[]{:S(2)}) collective-permute-start(s32[24]{0:T(128)S(1)} %get-tuple-element.331), channel_id=1, source_target_pairs={{16,0},{18,2},{20,4},{22,6},{24,8},{26,10},{28,12},{30,14},{0,16},... | collective-permute-start | bytes 296 | tf_op jit(solution)/shard_map/ppermute | solution.py:21
  38.2 5.9 %collective-permute-start.2 = (s32[24]{0:T(128)S(1)}, s32[24]{0:T(128)S(1)}, u32[]{:S(2)}, u32[]{:S(2)}) collective-permute-start(s32[24]{0:T(128)S(1)} %get-tuple-element.332), channel_id=1, source_target_pairs={{14,0},{16,2},{18,4},{20,6},{22,8},{24,10},{26,12},{28,14},{30,16}... | collective-permute-start | bytes 296 | tf_op jit(solution)/shard_map/ppermute | solution.py:21
  39.2 6.1 %collective-permute-start.3 = (s32[24]{0:T(128)S(1)}, s32[24]{0:T(128)S(1)}, u32[]{:S(2)}, u32[]{:S(2)}) collective-permute-start(s32[24]{0:T(128)S(1)} %get-tuple-element.333), channel_id=1, source_target_pairs={{2,0},{4,2},{6,4},{8,6},{10,8},{12,10},{14,12},{16,14},{18,16},{20... | collective-permute-start | bytes 296 | tf_op jit(solution)/shard_map/ppermute | solution.py:21
  44.1 7.2 %collective-permute-start.4 = (s32[24]{0:T(128)S(1)}, s32[24]{0:T(128)S(1)}, u32[]{:S(2)}, u32[]{:S(2)}) collective-permute-start(s32[24]{0:T(128)S(1)} %get-tuple-element.334), channel_id=1, source_target_pairs={{30,0},{0,2},{2,4},{4,6},{6,8},{8,10},{10,12},{12,14},{14,16},{16,... | collective-permute-start | bytes 296 | tf_op jit(solution)/shard_map/ppermute | solution.py:21
  45.4 6.4 %collective-permute-start.5 = (s32[24]{0:T(128)S(1)}, s32[24]{0:T(128)S(1)}, u32[]{:S(2)}, u32[]{:S(2)}) collective-permute-start(s32[24]{0:T(128)S(1)} %get-tuple-element.335), channel_id=1, source_target_pairs={{18,0},{20,2},{22,4},{24,6},{26,8},{28,10},{30,12},{0,14},{2,16},{... | collective-permute-start | bytes 296 | tf_op jit(solution)/shard_map/ppermute | solution.py:21
  51.2 4.5 %collective-permute-start.6 = (s32[24]{0:T(128)S(1)}, s32[24]{0:T(128)S(1)}, u32[]{:S(2)}, u32[]{:S(2)}) collective-permute-start(s32[24]{0:T(128)S(1)} %get-tuple-element.336), channel_id=1, source_target_pairs={{16,0},{18,2},{20,4},{22,6},{24,8},{26,10},{28,12},{30,14},{0,16},... | collective-permute-start | bytes 296 | tf_op jit(solution)/shard_map/ppermute | solution.py:21
  51.8 5.6 %collective-permute-start.7 = (s32[24]{0:T(128)S(1)}, s32[24]{0:T(128)S(1)}, u32[]{:S(2)}, u32[]{:S(2)}) collective-permute-start(s32[24]{0:T(128)S(1)} %get-tuple-element.330), channel_id=1, source_target_pairs={{14,0},{16,2},{18,4},{20,6},{22,8},{24,10},{26,12},{28,14},{30,16}... | collective-permute-start | bytes 296 | tf_op jit(solution)/shard_map/ppermute | solution.py:21
  55.7 9.0 %collective-permute-start.11 = (f32[24,9,128]{2,0,1:T(8,128)S(1)}, f32[24,9,128]{2,0,1:T(8,128)S(1)}, u32[]{:S(2)}, u32[]{:S(2)}) collective-permute-start(f32[24,9,128]{2,0,1:T(8,128)S(1)} %fusion.71), channel_id=1, source_target_pairs={{2,0},{4,2},{6,4},{8,6},{10,8},{12,10},{14,12},{16,14},{18,16},{20... | collective-permute-start | bytes 331784 | tf_op jit(solution)/shard_map/ppermute | solution.py:21
  57.4 9.5 %collective-permute-start.12 = (f32[24,9,128]{2,0,1:T(8,128)S(1)}, f32[24,9,128]{2,0,1:T(8,128)S(1)}, u32[]{:S(2)}, u32[]{:S(2)}) collective-permute-start(f32[24,9,128]{2,0,1:T(8,128)S(1)} %fusion.69), channel_id=1, source_target_pairs={{30,0},{0,2},{2,4},{4,6},{6,8},{8,10},{10,12},{12,14},{14,16},{16,... | collective-permute-start | bytes 331784 | tf_op jit(solution)/shard_map/ppermute | solution.py:21
  60.1 12.2 %collective-permute-start.13 = (f32[24,9,128]{2,0,1:T(8,128)S(1)}, f32[24,9,128]{2,0,1:T(8,128)S(1)}, u32[]{:S(2)}, u32[]{:S(2)}) collective-permute-start(f32[24,9,128]{2,0,1:T(8,128)S(1)} %fusion.67), channel_id=1, source_target_pairs={{18,0},{20,2},{22,4},{24,6},{26,8},{28,10},{30,12},{0,14},{2,16},{... | collective-permute-start | bytes 331784 | tf_op jit(solution)/shard_map/ppermute | solution.py:21
  62.1 10.4 %collective-permute-start.14 = (f32[24,9,128]{2,0,1:T(8,128)S(1)}, f32[24,9,128]{2,0,1:T(8,128)S(1)}, u32[]{:S(2)}, u32[]{:S(2)}) collective-permute-start(f32[24,9,128]{2,0,1:T(8,128)S(1)} %fusion.65), channel_id=1, source_target_pairs={{16,0},{18,2},{20,4},{22,6},{24,8},{26,10},{28,12},{30,14},{0,16},... | collective-permute-start | bytes 331784 | tf_op jit(solution)/shard_map/ppermute | solution.py:21
  63.9 9.9 %collective-permute-start.15 = (f32[24,9,128]{2,0,1:T(8,128)S(1)}, f32[24,9,128]{2,0,1:T(8,128)S(1)}, u32[]{:S(2)}, u32[]{:S(2)}) collective-permute-start(f32[24,9,128]{2,0,1:T(8,128)S(1)} %fusion.63), channel_id=1, source_target_pairs={{14,0},{16,2},{18,4},{20,6},{22,8},{24,10},{26,12},{28,14},{30,16}... | collective-permute-start | bytes 331784 | tf_op jit(solution)/shard_map/ppermute | solution.py:21
  64.7 9.1 %copy-start.4 = (f32[192,2]{0,1:T(2,128)S(1)}, f32[192,2]{0,1:T(2,128)}, u32[]{:S(2)}) copy-start(f32[192,2]{0,1:T(2,128)} %constant.270) | copy-start | bytes 4612
  74.4 50.0 %copy-start.1 = (f32[64,128]{1,0:T(8,128)S(1)}, f32[64,128]{1,0:T(8,128)}, u32[]{:S(2)}) copy-start(f32[64,128]{1,0:T(8,128)} %param.16) | copy-start | bytes 98308
  74.4 50.0 %copy-start.2 = (f32[64,128]{1,0:T(8,128)S(1)}, f32[64,128]{1,0:T(8,128)}, u32[]{:S(2)}) copy-start(f32[64,128]{1,0:T(8,128)} %param.17) | copy-start | bytes 98308
  125.9 6.8 %collective-permute-start.16 = (f32[24,128]{1,0:T(8,128)S(1)}, f32[24,128]{1,0:T(8,128)S(1)}, u32[]{:S(2)}, u32[]{:S(2)}) collective-permute-start(f32[24,128]{1,0:T(8,128)S(1)} %fusion.106), channel_id=1, source_target_pairs={{18,0},{20,2},{22,4},{24,6},{26,8},{28,10},{30,12},{0,14},{2,16},{... | collective-permute-start | bytes 36872 | tf_op jit(solution)/shard_map/ppermute | solution.py:21
  126.1 9.2 %collective-permute-start.17 = (f32[24,128]{1,0:T(8,128)S(1)}, f32[24,128]{1,0:T(8,128)S(1)}, u32[]{:S(2)}, u32[]{:S(2)}) collective-permute-start(f32[24,128]{1,0:T(8,128)S(1)} %fusion.104), channel_id=1, source_target_pairs={{16,0},{18,2},{20,4},{22,6},{24,8},{26,10},{28,12},{30,14},{0,16},... | collective-permute-start | bytes 36872 | tf_op jit(solution)/shard_map/ppermute | solution.py:21
  126.2 12.4 %collective-permute-start.18 = (f32[24,128]{1,0:T(8,128)S(1)}, f32[24,128]{1,0:T(8,128)S(1)}, u32[]{:S(2)}, u32[]{:S(2)}) collective-permute-start(f32[24,128]{1,0:T(8,128)S(1)} %fusion.102), channel_id=1, source_target_pairs={{14,0},{16,2},{18,4},{20,6},{22,8},{24,10},{26,12},{28,14},{30,16}... | collective-permute-start | bytes 36872 | tf_op jit(solution)/shard_map/ppermute | solution.py:21
  130.2 9.1 %collective-permute-start.19 = (f32[24,128]{1,0:T(8,128)S(1)}, f32[24,128]{1,0:T(8,128)S(1)}, u32[]{:S(2)}, u32[]{:S(2)}) collective-permute-start(f32[24,128]{1,0:T(8,128)S(1)} %fusion.100), channel_id=1, source_target_pairs={{2,0},{4,2},{6,4},{8,6},{10,8},{12,10},{14,12},{16,14},{18,16},{20... | collective-permute-start | bytes 36872 | tf_op jit(solution)/shard_map/ppermute | solution.py:21
  132.4 7.3 %collective-permute-start.20 = (f32[24,128]{1,0:T(8,128)S(1)}, f32[24,128]{1,0:T(8,128)S(1)}, u32[]{:S(2)}, u32[]{:S(2)}) collective-permute-start(f32[24,128]{1,0:T(8,128)S(1)} %fusion.98), channel_id=1, source_target_pairs={{30,0},{0,2},{2,4},{4,6},{6,8},{8,10},{10,12},{12,14},{14,16},{16,... | collective-permute-start | bytes 36872 | tf_op jit(solution)/shard_map/ppermute | solution.py:21
  132.6 7.1 %collective-permute-start.21 = (f32[24,128]{1,0:T(8,128)S(1)}, f32[24,128]{1,0:T(8,128)S(1)}, u32[]{:S(2)}, u32[]{:S(2)}) collective-permute-start(f32[24,128]{1,0:T(8,128)S(1)} %fusion.96), channel_id=1, source_target_pairs={{18,0},{20,2},{22,4},{24,6},{26,8},{28,10},{30,12},{0,14},{2,16},{... | collective-permute-start | bytes 36872 | tf_op jit(solution)/shard_map/ppermute | solution.py:21
  135.3 5.0 %collective-permute-start.22 = (f32[24,128]{1,0:T(8,128)S(1)}, f32[24,128]{1,0:T(8,128)S(1)}, u32[]{:S(2)}, u32[]{:S(2)}) collective-permute-start(f32[24,128]{1,0:T(8,128)S(1)} %fusion.94), channel_id=1, source_target_pairs={{16,0},{18,2},{20,4},{22,6},{24,8},{26,10},{28,12},{30,14},{0,16},... | collective-permute-start | bytes 36872 | tf_op jit(solution)/shard_map/ppermute | solution.py:21
  138.6 5.5 %collective-permute-start.23 = (f32[24,128]{1,0:T(8,128)S(1)}, f32[24,128]{1,0:T(8,128)S(1)}, u32[]{:S(2)}, u32[]{:S(2)}) collective-permute-start(f32[24,128]{1,0:T(8,128)S(1)} %fusion.92), channel_id=1, source_target_pairs={{14,0},{16,2},{18,4},{20,6},{22,8},{24,10},{26,12},{28,14},{30,16}... | collective-permute-start | bytes 36872 | tf_op jit(solution)/shard_map/ppermute | solution.py:21
  223.2 0.7 copy-start
Sparse Core Ops, SparseCore 0:
  224.0 14.1 all-reduce.2
where the time goes:
time: 249 us; the launch traced here: 248 us
  matrix products  68.5 us (28%)
  other arithmetic  61.5 us (25%)
  starting transfers between devices  46.6 us (19%)
  waiting for transfers between devices  32.9 us (13%)
  between operations  16.5 us (7%)
  local copies, waits for them, and re-layouts  11.8 us (5%)
  blocking collectives  7.05 us (3%)
  loops' own time  3.17 us (1%)
    dot_general x124, matrix products, pick_rows(): jnp.dot(equal.astype(jnp.float32), flat, precision=lax.Precision.HIGHEST)  58.3 us
    ppermute x24, starting transfers between devices, passed_along(): return lax.ppermute(block, axis, route)  46.5 us
    ppermute x24, waiting for transfers between devices, passed_along(): return lax.ppermute(block, axis, route)  18.7 us
    mul x18, other arithmetic, pair_force(): weight * (press_target * slope_target + press_source * slope_source + vis...  14.2 us
    psum x1, waiting for transfers between devices, local(): forces = lax.psum(partial_force, 'task')  14.2 us
    reduce_sum x36, other arithmetic, geometry(): dist_sq = jnp.sum(separation * separation, axis=0)  13.8 us
    dot_general x36, matrix products, one_turn(): jnp.tensordot(selector, pieces, axes=1, precision=lax.Precision.HIGHEST)  10.2 us
    reduce_sum x18, other arithmetic, pair_force(): accel = -jnp.sum(pull[None] * separation, axis=2)  9.45 us
  transfers between devices with their start and end apart: 25, of which 11 were waited for; matrix products, arithmetic and copies ran while one was open for 3% of the time, Pallas kernels for 0%

commit v1 on v0

v1 whole, which is shorter than its diff:
```python
import math

import jax
import jax.numpy as jnp
from jax import lax
from jax.experimental import pallas as pl
from jax.experimental.pallas import tpu as pltpu
from jax.sharding import PartitionSpec as P

GY = 8


GAMMA = 5.0 / 3.0
VISC_ALPHA = 0.8
KERNEL_NORM = 8.0 / math.pi
DIRECTIONS = ((-1, -1), (-1, 0), (-1, 1), (0, -1), (0, 1), (1, -1), (1, 0), (1, 1))
SUB = 8


def passed_along(block, axis, distance):
    devices = range(lax.axis_size(axis))
    route = [((i - distance) % len(devices), i) for i in devices]
    return lax.ppermute(block, axis, route)


def fetch_ghosts(own, send_rows):
    per_direction = send_rows.shape[1]
    picked = jnp.take(own, send_rows.reshape(-1), axis=0, mode="clip")
    picked = picked.reshape((len(DIRECTIONS), per_direction) + own.shape[1:])
    arrived = [
        passed_along(picked[number], "dom", col_step * GY + row_step)
        for number, (col_step, row_step) in enumerate(DIRECTIONS)
    ]
    return jnp.concatenate(arrived, axis=0)


def place_ghosts(ghost_feat, per_direction):
    shifts = []
    for col_step, row_step in DIRECTIONS:
        shifts += [(float(col_step), float(row_step))] * per_direction
    offsets = jnp.asarray(shifts, dtype=ghost_feat.dtype)
    shifted = ghost_feat[:, 0:2, :] - offsets[:, :, None]
    return jnp.concatenate([shifted, ghost_feat[:, 2:, :]], axis=1)


def pick_tasks(task_lists, task_counts):
    both_lists, both_counts = (
        lax.all_gather(task_lists, "task", axis=1, tiled=True),
        lax.all_gather(task_counts, "task", axis=1, tiled=True),
    )
    list_pair = both_lists[0]
    count_pair = both_counts[0]
    capacity = list_pair.shape[1]
    overall = count_pair[0] + count_pair[1]
    member_rank = lax.axis_index("task")
    my_count = (overall + 1 - member_rank) // 2
    places = 2 * jnp.arange(capacity, dtype=jnp.int32) + member_rank
    first_pick = list_pair[0][jnp.clip(places, 0, capacity - 1)]
    second_pick = list_pair[1][jnp.clip(places - count_pair[0], 0, capacity - 1)]
    my_list = jnp.where(places < count_pair[0], first_pick, second_pick)
    return (my_list, my_count)


def spread(row):
    return jnp.broadcast_to(row, (SUB, row.shape[-1]))


def turned(value, tile):
    return pltpu.roll(value, tile * SUB, 1, stride=1, stride_axis=0)


def density_kernel(task_ref, count_ref, feat_ref, out_ref):
    source_total = feat_ref.shape[0]
    lanes = feat_ref.shape[2]
    out_ref[...] = jnp.zeros(out_ref.shape, out_ref.dtype)
    first_row = lax.broadcasted_iota(jnp.int32, (SUB, lanes), 0) == 0

    def one_task(n, carry):
        value = task_ref[n]
        target = value // source_total
        source = value % source_total
        tb = feat_ref[target]
        sb = feat_ref[source]
        xi = spread(tb[0:1])
        yi = spread(tb[1:2])
        zi = spread(tb[2:3])
        hinv = spread(1.0 / tb[7:8])
        xs = spread(sb[0:1])
        ys = spread(sb[1:2])
        zs = spread(sb[2:3])
        ms = spread(sb[6:7])
        acc = jnp.zeros((SUB, lanes), jnp.float32)
        for tile in range(lanes // SUB):
            dx = xi - turned(xs, tile)
            dy = yi - turned(ys, tile)
            dz = zi - turned(zs, tile)
            q = jnp.sqrt(dx * dx + dy * dy + dz * dz) * hinv
            q2 = q * q
            inner = 1.0 + q2 * (6.0 * q - 6.0)
            om = jnp.maximum(1.0 - q, 0.0)
            outer = 2.0 * (om * om * om)
            term = turned(ms, tile) * jnp.where(q < 0.5, inner, outer)
            if tile == 0:
                term = jnp.where(jnp.logical_and(first_row, target == source), 0.0, term)
            acc = acc + term
        out_ref[target] = out_ref[target] + acc
        return carry

    lax.fori_loop(0, count_ref[0], one_task, 0)


def force_rows(block):
    h = block[7:8]
    hinv = 1.0 / h
    h2 = h * h
    g5 = KERNEL_NORM / (h2 * h2 * h)
    energy = block[8:9]
    rho = block[9:10]
    pr = (GAMMA - 1.0) * energy / rho
    half_sound = 0.5 * jnp.sqrt(GAMMA * (GAMMA - 1.0) * energy)
    return dict(
        x=block[0:1], y=block[1:2], z=block[2:3],
        vx=block[3:4], vy=block[4:5], vz=block[5:6],
        m=block[6:7], hh=0.5 * h, hinv=hinv, g5=g5, pr=pr,
        cs=half_sound, rh=0.5 * rho,
    )


def force_kernel(task_ref, count_ref, feat_ref, out_ref):
    source_total = feat_ref.shape[0]
    lanes = feat_ref.shape[2]
    out_ref[...] = jnp.zeros(out_ref.shape, out_ref.dtype)
    first_row = lax.broadcasted_iota(jnp.int32, (SUB, lanes), 0) == 0

    def one_task(n, carry):
        value = task_ref[n]
        target = value // source_total
        source = value % source_total
        ti = {k: spread(v) for k, v in force_rows(feat_ref[target]).items()}
        sj = {k: spread(v) for k, v in force_rows(feat_ref[source]).items()}
        ax = jnp.zeros((SUB, lanes), jnp.float32)
        ay = ax
        az = ax
        heat = ax
        for tile in range(lanes // SUB):
            s = {k: turned(v, tile) for k, v in sj.items()}
            dx = ti["x"] - s["x"]
            dy = ti["y"] - s["y"]
            dz = ti["z"] - s["z"]
            dist_sq = dx * dx + dy * dy + dz * dz
            approach = (ti["vx"] - s["vx"]) * dx + (ti["vy"] - s["vy"]) * dy + (ti["vz"] - s["vz"]) * dz
            radius = jnp.sqrt(dist_sq)
            rinv = 1.0 / radius

            def slope(q, hh):
                om = jnp.maximum(1.0 - q, 0.0)
                return jnp.where(q < 0.5, 18.0 * q - 12.0, (-12.0 * rinv) * (om * om * hh))

            gi = ti["g5"] * slope(radius * ti["hinv"], ti["hh"])
            gj = s["g5"] * slope(radius * s["hinv"], s["hh"])
            hb = ti["hh"] + s["hh"]
            den = dist_sq + 0.01 * (hb * hb)
            lean = hb * jnp.minimum(approach, 0.0)
            sound = ti["cs"] + s["cs"]
            rho_mean = ti["rh"] + s["rh"]
            visc = lean * (2.0 * VISC_ALPHA * lean - VISC_ALPHA * sound * den) / ((den * den) * rho_mean)
            vg = visc * (0.5 * (gi + gj))
            press = ti["pr"] * gi
            weight = s["m"]
            if tile == 0:
                weight = jnp.where(jnp.logical_and(first_row, target == source), 0.0, weight)
            pull = weight * (press + s["pr"] * gj + vg)
            ax = ax + pull * dx
            ay = ay + pull * dy
            az = az + pull * dz
            heat = heat + weight * (press + 0.5 * vg) * approach
        out_ref[target, 0] = out_ref[target, 0] + ax
        out_ref[target, 1] = out_ref[target, 1] + ay
        out_ref[target, 2] = out_ref[target, 2] + az
        out_ref[target, 3] = out_ref[target, 3] + heat
        return carry

    lax.fori_loop(0, count_ref[0], one_task, 0)


def run_kernel(kernel, my_list, my_count, feat, out_shape):
    smem = pl.BlockSpec(memory_space=pltpu.SMEM)
    vmem = pl.BlockSpec(memory_space=pltpu.VMEM)
    return pl.pallas_call(
        kernel,
        out_shape=jax.ShapeDtypeStruct(out_shape, jnp.float32),
        in_specs=[smem, smem, vmem],
        out_specs=vmem,
    )(my_list, jnp.reshape(my_count, (1,)).astype(jnp.int32), feat)


def local(
    positions,
    velocities,
    masses,
    smoothing,
    energy,
    block_counts,
    send_lists,
    task_lists,
    task_counts,
):
    own_count = positions.shape[0]
    block_width = positions.shape[2]
    valid = jnp.arange(block_width, dtype=jnp.int32)[None, :] < block_counts[:, None]
    live_mass = jnp.where(valid, masses, 0.0)
    own_feat = jnp.concatenate(
        [positions, velocities, live_mass[:, None], smoothing[:, None], energy[:, None]], axis=1
    )
    send_rows = send_lists[0]
    ghost_feat = place_ghosts(fetch_ghosts(own_feat, send_rows), send_rows.shape[1])
    all_feat = jnp.concatenate([own_feat, ghost_feat], axis=0)
    my_list, my_count = pick_tasks(task_lists, task_counts)

    partial_rho = run_kernel(
        density_kernel, my_list, my_count, all_feat, (own_count, SUB, block_width)
    )
    partial_rho = KERNEL_NORM / smoothing**3 * jnp.sum(partial_rho, axis=1)
    rho_own = lax.psum(partial_rho, "task") + masses * KERNEL_NORM / smoothing**3
    ghost_rho = fetch_ghosts(rho_own, send_rows)
    all_rho = jnp.concatenate([rho_own, ghost_rho], axis=0)
    force_feat = jnp.concatenate([all_feat, all_rho[:, None]], axis=1)

    partial_force = run_kernel(
        force_kernel, my_list, my_count, force_feat, (own_count, 4, SUB, block_width)
    )
    forces = lax.psum(jnp.sum(partial_force, axis=2), "task")
    density = jnp.where(valid, rho_own, 0.0)
    acceleration = jnp.where(valid[:, None, :], -forces[:, 0:3], 0.0)
    energy_rate = jnp.where(valid, forces[:, 3], 0.0)
    return (density, acceleration, energy_rate)


def solution(mesh):
    placed = (
        P("dom", None, None),
        P("dom", None, None),
        P("dom", None),
        P("dom", None),
        P("dom", None),
        P("dom"),
        P("dom", None, None),
        P("dom", "task", None),
        P("dom", "task"),
    )
    return jax.shard_map(
        local,
        mesh=mesh,
        in_specs=placed,
        out_specs=(P("dom", None), P("dom", None, None), P("dom", None)),
        check_vma=False,
    )
```

time: 249 us -> 165 us (0.66)
  matrix products: 68.5 us -> 0 us
  other arithmetic: 61.5 us -> 11.9 us
  Pallas kernels: 0 us -> 36.1 us
  loops' own time: 3.17 us -> 0 us
    dot_general x160 -> x0, matrix products: 68.5 us -> none  [the longest x124 58.3 us: pick_rows(): jnp.dot(equal.astype(jnp.float32), flat, precision=lax.Precision.HIGHEST)]
    pallas_call x0 -> x2, Pallas kernels: none -> 36.1 us  [run_kernel(): pl.pallas_call(kernel, out_shape=jax.ShapeDtypeStruct(out_shape, jnp.floa...]
    reduce_sum x109 -> x2, other arithmetic: 37.1 us -> 2.53 us  [the longest x1 1.51 us: local(): forces = lax.psum(jnp.sum(partial_force, axis=2), 'task')]
    mul x18 -> x1, other arithmetic: 14.2 us -> 0.02 us  [local(): partial_rho = KERNEL_NORM / smoothing ** 3 * jnp.sum(partial_rho, axis=1)]
    another operation x2 -> x0, loops' own time: 3.17 us -> none  [run_tasks(): return lax.fori_loop(0, rounds, one_turn, start_value)]
    lt x36 -> x0, other arithmetic: 2.73 us -> none  [active_flags(): present = column[None, :] < source_particle_count]
    unnamed x36 -> x31, local copies, waits for them, and re-layouts: 5.69 us -> 3.34 us
    ppermute x24 -> x16, starting transfers between devices: 46.5 us -> 45.8 us  [passed_along(): return lax.ppermute(block, axis, route)]
  transfers between devices with their start and end apart: 25 -> 17, of which waited for: 11 -> 8; matrix products, arithmetic and copies ran while one was open for 3% -> 4% of each run, Pallas kernels for 0% -> 0%
where the time goes in v1:
time: 165 us; the launch traced here: 164 us
  starting transfers between devices  45.9 us (28%)
  Pallas kernels  36.1 us (22%)
  waiting for transfers between devices  34.6 us (21%)
  between operations  16.3 us (10%)
  local copies, waits for them, and re-layouts  12 us (7%)
  other arithmetic  11.9 us (7%)
  blocking collectives  7.04 us (4%)
    ppermute x16, starting transfers between devices, passed_along(): return lax.ppermute(block, axis, route)  45.8 us
    pallas_call x2, Pallas kernels, run_kernel(): pl.pallas_call(kernel, out_shape=jax.ShapeDtypeStruct(out_shape, jnp.floa...  36.1 us
    ppermute x16, waiting for transfers between devices, passed_along(): return lax.ppermute(block, axis, route)  18.6 us
    psum x1, waiting for transfers between devices, local(): forces = lax.psum(jnp.sum(partial_force, axis=2), 'task')  16 us
    psum x1, blocking collectives, local(): lax.psum(partial_rho, 'task') + masses * KERNEL_NORM / smoothing ** 3  3.41 us
    unnamed x31, local copies, waits for them, and re-layouts  3.34 us
  transfers between devices with their start and end apart: 17, of which 8 were waited for; matrix products, arithmetic and copies ran while one was open for 4% of the time, Pallas kernels for 0%

profile of v1, /device:TPU:0, one launch (start us, length us, event | category | flops | bytes accessed | tf_op | source)
XLA Modules:
  0.0 163.9 jit_solution(3920930178483476644)
XLA Ops:
  10.8 1.8 %concatenate.18 = f32[64,9,128]{2,1,0:T(8,128)S(1)} concatenate(f32[64,3,128]{2,1,0:T(4,128)S(1)} %copy.20, f32[64,3,128]{2,1,0:T(4,128)S(1)} %copy.21, f32[64,1,128]{2,1,0:T(1,128)S(1)} %bitcast.28, f32[64,1,128]{2,1,0:T(1,128)} %bitcast.26, f32[64,1,128]{2,1,0:T(1,128)} %bitcast.29), dimensions={1} | concatenate | bytes 589824 | tf_op jit(solution)/shard_map/concatenate | solution.py:212
  14.2 4.9 %collective-permute-start = (f32[24,9,128]{2,1,0:T(8,128)}, f32[24,9,128]{2,1,0:T(8,128)S(1)}, u32[]{:S(2)}, u32[]{:S(2)}) collective-permute-start(f32[24,9,128]{2,1,0:T(8,128)} %get-tuple-element.12), channel_id=1, source_target_pairs={{18,0},{20,2},{22,4},{24,6},{26,8},{28,10},{30,12},{0,14},{2,16},{... | collective-permute-start | bytes 331784 | tf_op jit(solution)/shard_map/ppermute | solution.py:23
  19.2 2.6 %collective-permute-start.1 = (f32[24,9,128]{2,1,0:T(8,128)S(1)}, f32[24,9,128]{2,1,0:T(8,128)S(1)}, u32[]{:S(2)}, u32[]{:S(2)}) collective-permute-start(f32[24,9,128]{2,1,0:T(8,128)S(1)} %get-tuple-element.11), channel_id=1, source_target_pairs={{16,0},{18,2},{20,4},{22,6},{24,8},{26,10},{28,12},{30,14},{0,16},... | collective-permute-start | bytes 331784 | tf_op jit(solution)/shard_map/ppermute | solution.py:23
  22.1 3.2 %collective-permute-start.3 = (f32[24,9,128]{2,1,0:T(8,128)S(1)}, f32[24,9,128]{2,1,0:T(8,128)S(1)}, u32[]{:S(2)}, u32[]{:S(2)}) collective-permute-start(f32[24,9,128]{2,1,0:T(8,128)S(1)} %get-tuple-element.9), channel_id=1, source_target_pairs={{2,0},{4,2},{6,4},{8,6},{10,8},{12,10},{14,12},{16,14},{18,16},{20... | collective-permute-start | bytes 331784 | tf_op jit(solution)/shard_map/ppermute | solution.py:23
  25.4 1.8 %all_gather.7 = s32[1,2,128]{2,0,1:T(1,128)S(1)} all-gather(s32[1,1,128]{2,0,1:T(1,128)S(1)} %bitcast.31), channel_id=1, replica_groups=mesh['dom'=16,'task'=2] {'task'}, dimensions={1}, use_global_device_ids=true | all-gather | bytes 1536 | tf_op jit(solution)/shard_map/all_gather | solution.py:48
  29.1 1.8 %all-reduce = s32[2]{0:T(128)S(1)} all-reduce(s32[2]{0:T(128)S(1)} %bitcast_dynamic-update-slice_fusion), channel_id=1, replica_groups=mesh['dom'=16,'task'=2] {'task'}, use_global_device_ids=true, to_apply=%add | all-reduce | flops 2 | bytes 16
  32.2 1.2 gather_fusion
  33.4 1.2 gather_fusion.1
  34.7 1.2 compare_select_fusion.2.task_ref
  37.8 3.4 %collective-permute-start.5 = (f32[24,9,128]{2,1,0:T(8,128)S(1)}, f32[24,9,128]{2,1,0:T(8,128)S(1)}, u32[]{:S(2)}, u32[]{:S(2)}) collective-permute-start(f32[24,9,128]{2,1,0:T(8,128)S(1)} %get-tuple-element.7), channel_id=1, source_target_pairs={{18,0},{20,2},{22,4},{24,6},{26,8},{28,10},{30,12},{0,14},{2,16},{... | collective-permute-start | bytes 331784 | tf_op jit(solution)/shard_map/ppermute | solution.py:23
  41.3 2.2 %collective-permute-start.6 = (f32[24,9,128]{2,1,0:T(8,128)S(1)}, f32[24,9,128]{2,1,0:T(8,128)S(1)}, u32[]{:S(2)}, u32[]{:S(2)}) collective-permute-start(f32[24,9,128]{2,1,0:T(8,128)S(1)} %get-tuple-element.6), channel_id=1, source_target_pairs={{16,0},{18,2},{20,4},{22,6},{24,8},{26,10},{28,12},{30,14},{0,16},... | collective-permute-start | bytes 331784 | tf_op jit(solution)/shard_map/ppermute | solution.py:23
  43.5 6.5 %collective-permute-start.7 = (f32[24,9,128]{2,1,0:T(8,128)S(1)}, f32[24,9,128]{2,1,0:T(8,128)S(1)}, u32[]{:S(2)}, u32[]{:S(2)}) collective-permute-start(f32[24,9,128]{2,1,0:T(8,128)S(1)} %get-tuple-element.5), channel_id=1, source_target_pairs={{14,0},{16,2},{18,4},{20,6},{22,8},{24,10},{26,12},{28,14},{30,16}... | collective-permute-start | bytes 331784 | tf_op jit(solution)/shard_map/ppermute | solution.py:23
  50.1 8.8 %collective-permute-done.5 = f32[24,9,128]{2,1,0:T(8,128)S(1)} collective-permute-done((f32[24,9,128]{2,1,0:T(8,128)S(1)}, f32[24,9,128]{2,1,0:T(8,128)S(1)}, u32[]{:S(2)}, u32[]{:S(2)}) %collective-permute-start.5) | collective-permute-done | bytes 110624 | tf_op jit(solution)/shard_map/ppermute | solution.py:23
  58.9 1.5 collective-permute-done.6
  60.4 2.2 %collective-permute-done.7 = f32[24,9,128]{2,1,0:T(8,128)S(1)} collective-permute-done((f32[24,9,128]{2,1,0:T(8,128)S(1)}, f32[24,9,128]{2,1,0:T(8,128)S(1)}, u32[]{:S(2)}, u32[]{:S(2)}) %collective-permute-start.7) | collective-permute-done | bytes 110624 | tf_op jit(solution)/shard_map/ppermute | solution.py:23
  63.0 1.6 maximum_maximum_fusion.feat_ref
  64.6 12.7 %shard_map.121 = f32[64,8,128]{2,1,0:T(8,128)} custom-call(s32[128]{0:T(128)} %compare_select_fusion.2.task_ref, s32[1]{0:T(128)} %bitcast.10.count_ref, f32[256,9,128]{2,1,0:T(8,128)} %maximum_maximum_fusion.feat_ref), custom_call_target="tpu_custom_call" | custom-call | tf_op jit(solution)/shard_map/pallas_call | solution.py:189
  78.4 3.4 %psum.14 = f32[64,128]{1,0:T(8,128)S(1)} all-reduce(f32[64,128]{1,0:T(8,128)S(1)} %divide_multiply_fusion), channel_id=1, replica_groups=mesh['dom'=16,'task'=2] {'task'}, use_global_device_ids=true, to_apply=%region_1.2 | all-reduce | flops 8192 | bytes 65536 | tf_op jit(solution)/shard_map/psum | solution.py:224
  82.6 4.2 %collective-permute-start.8 = (f32[24,128]{1,0:T(8,128)S(1)}, f32[24,128]{1,0:T(8,128)S(1)}, u32[]{:S(2)}, u32[]{:S(2)}) collective-permute-start(f32[24,128]{1,0:T(8,128)S(1)} %get-tuple-element.20), channel_id=1, source_target_pairs={{18,0},{20,2},{22,4},{24,6},{26,8},{28,10},{30,12},{0,14},{2,16},{... | collective-permute-start | bytes 36872 | tf_op jit(solution)/shard_map/ppermute | solution.py:23
  86.7 9.0 %collective-permute-start.9 = (f32[24,128]{1,0:T(8,128)S(1)}, f32[24,128]{1,0:T(8,128)S(1)}, u32[]{:S(2)}, u32[]{:S(2)}) collective-permute-start(f32[24,128]{1,0:T(8,128)S(1)} %get-tuple-element.19), channel_id=1, source_target_pairs={{16,0},{18,2},{20,4},{22,6},{24,8},{26,10},{28,12},{30,14},{0,16},... | collective-permute-start | bytes 36872 | tf_op jit(solution)/shard_map/ppermute | solution.py:23
  95.7 3.3 %collective-permute-start.11 = (f32[24,128]{1,0:T(8,128)S(1)}, f32[24,128]{1,0:T(8,128)S(1)}, u32[]{:S(2)}, u32[]{:S(2)}) collective-permute-start(f32[24,128]{1,0:T(8,128)S(1)} %get-tuple-element.17), channel_id=1, source_target_pairs={{2,0},{4,2},{6,4},{8,6},{10,8},{12,10},{14,12},{16,14},{18,16},{20... | collective-permute-start | bytes 36872 | tf_op jit(solution)/shard_map/ppermute | solution.py:23
  99.0 4.4 %collective-permute-start.13 = (f32[24,128]{1,0:T(8,128)S(1)}, f32[24,128]{1,0:T(8,128)S(1)}, u32[]{:S(2)}, u32[]{:S(2)}) collective-permute-start(f32[24,128]{1,0:T(8,128)S(1)} %get-tuple-element.15), channel_id=1, source_target_pairs={{18,0},{20,2},{22,4},{24,6},{26,8},{28,10},{30,12},{0,14},{2,16},{... | collective-permute-start | bytes 36872 | tf_op jit(solution)/shard_map/ppermute | solution.py:23
  103.3 1.8 %collective-permute-start.14 = (f32[24,128]{1,0:T(8,128)S(1)}, f32[24,128]{1,0:T(8,128)S(1)}, u32[]{:S(2)}, u32[]{:S(2)}) collective-permute-start(f32[24,128]{1,0:T(8,128)S(1)} %get-tuple-element.14), channel_id=1, source_target_pairs={{16,0},{18,2},{20,4},{22,6},{24,8},{26,10},{28,12},{30,14},{0,16},... | collective-permute-start | bytes 36872 | tf_op jit(solution)/shard_map/ppermute | solution.py:23
  105.2 1.2 collective-permute-done.12
  106.4 1.6 collective-permute-done.14
  107.9 2.7 %collective-permute-done.15 = f32[24,128]{1,0:T(8,128)S(1)} collective-permute-done((f32[24,128]{1,0:T(8,128)S(1)}, f32[24,128]{1,0:T(8,128)S(1)}, u32[]{:S(2)}, u32[]{:S(2)}) %collective-permute-start.15) | collective-permute-done | bytes 12320 | tf_op jit(solution)/shard_map/ppermute | solution.py:23
  110.7 1.7 %pad_maximum_fusion.feat_ref = f32[256,10,128]{2,1,0:T(8,128)} fusion(f32[256,1,128]{2,1,0:T(1,128)S(1)} %bitcast.27, f32[192,7,128]{2,1,0:T(8,128)S(1)} %slice.137, f32[192,2,128]{2,1,0:T(2,128)S(1)} %slice_add_fusion, f32[64,9,128]{2,1,0:T(8,128)S(1)} %concatenate.18), kind=kLoop, calls=%fused_computation.5 | loop fusion | flops 983040 | bytes 2621440 | tf_op jit(solution)/shard_map/concatenate | solution.py:227
  112.4 23.4 %shard_map.122 = f32[64,4,8,128]{3,2,1,0:T(8,128)} custom-call(s32[128]{0:T(128)} %compare_select_fusion.2.task_ref, s32[1]{0:T(128)} %bitcast.10.count_ref, f32[256,10,128]{2,1,0:T(8,128)} %pad_maximum_fusion.feat_ref), custom_call_target="tpu_custom_call" | custom-call | tf_op jit(solution)/shard_map/pallas_call | solution.py:189
  135.8 1.5 reduce_sum.19
  138.1 16.0 %all-reduce.3.cloned.1.call-done = f32[64,4,128]{2,0,1:T(8,128)} async-done(((f32[64,4,128]{2,0,1:T(8,128)}), f32[64,4,128]{2,0,1:T(8,128)}) %all-reduce.3.cloned.1.call-update) | async-done | bytes 131088 | tf_op jit(solution)/shard_map/psum | solution.py:232
  154.1 1.5 fusion.1
  155.5 1.5 fusion
  (69 shorter events, 11.8 us)
Async XLA Ops:
  7.2 146.9 %all-reduce.3.cloned.1.call-start = ((), (), s32[]{:S(2)}) async-start(), calls=%async_computation | async-start | bytes 262144 | tf_op jit(solution)/shard_map/psum | solution.py:232
  13.4 11.9 %copy-start.4 = (s32[1,1,128]{2,1,0:T(1,128)S(1)}, s32[1,1,128]{2,1,0:T(1,128)}, u32[]{:S(2)}) copy-start(s32[1,1,128]{2,1,0:T(1,128)} %param.17) | copy-start | bytes 1540
  13.4 14.4 %copy-start.5 = (u32[32]{0:T(128)S(1)}, u32[32]{0:T(128)}, u32[]{:S(2)}) copy-start(u32[32]{0:T(128)} %constant.40) | copy-start | bytes 388
  14.2 23.6 %collective-permute-start = (f32[24,9,128]{2,1,0:T(8,128)}, f32[24,9,128]{2,1,0:T(8,128)S(1)}, u32[]{:S(2)}, u32[]{:S(2)}) collective-permute-start(f32[24,9,128]{2,1,0:T(8,128)} %get-tuple-element.12), channel_id=1, source_target_pairs={{18,0},{20,2},{22,4},{24,6},{26,8},{28,10},{30,12},{0,14},{2,16},{... | collective-permute-start | bytes 331784 | tf_op jit(solution)/shard_map/ppermute | solution.py:23
  19.2 22.1 %collective-permute-start.1 = (f32[24,9,128]{2,1,0:T(8,128)S(1)}, f32[24,9,128]{2,1,0:T(8,128)S(1)}, u32[]{:S(2)}, u32[]{:S(2)}) collective-permute-start(f32[24,9,128]{2,1,0:T(8,128)S(1)} %get-tuple-element.11), channel_id=1, source_target_pairs={{16,0},{18,2},{20,4},{22,6},{24,8},{26,10},{28,12},{30,14},{0,16},... | collective-permute-start | bytes 331784 | tf_op jit(solution)/shard_map/ppermute | solution.py:23
  21.8 21.8 %collective-permute-start.2 = (f32[24,9,128]{2,1,0:T(8,128)S(1)}, f32[24,9,128]{2,1,0:T(8,128)S(1)}, u32[]{:S(2)}, u32[]{:S(2)}) collective-permute-start(f32[24,9,128]{2,1,0:T(8,128)S(1)} %get-tuple-element.10), channel_id=1, source_target_pairs={{14,0},{16,2},{18,4},{20,6},{22,8},{24,10},{26,12},{28,14},{30,16}... | collective-permute-start | bytes 331784 | tf_op jit(solution)/shard_map/ppermute | solution.py:23
  22.1 27.9 %collective-permute-start.3 = (f32[24,9,128]{2,1,0:T(8,128)S(1)}, f32[24,9,128]{2,1,0:T(8,128)S(1)}, u32[]{:S(2)}, u32[]{:S(2)}) collective-permute-start(f32[24,9,128]{2,1,0:T(8,128)S(1)} %get-tuple-element.9), channel_id=1, source_target_pairs={{2,0},{4,2},{6,4},{8,6},{10,8},{12,10},{14,12},{16,14},{18,16},{20... | collective-permute-start | bytes 331784 | tf_op jit(solution)/shard_map/ppermute | solution.py:23
  25.4 24.7 %collective-permute-start.4 = (f32[24,9,128]{2,1,0:T(8,128)S(1)}, f32[24,9,128]{2,1,0:T(8,128)S(1)}, u32[]{:S(2)}, u32[]{:S(2)}) collective-permute-start(f32[24,9,128]{2,1,0:T(8,128)S(1)} %get-tuple-element.8), channel_id=1, source_target_pairs={{30,0},{0,2},{2,4},{4,6},{6,8},{8,10},{10,12},{12,14},{14,16},{16,... | collective-permute-start | bytes 331784 | tf_op jit(solution)/shard_map/ppermute | solution.py:23
  37.8 21.1 %collective-permute-start.5 = (f32[24,9,128]{2,1,0:T(8,128)S(1)}, f32[24,9,128]{2,1,0:T(8,128)S(1)}, u32[]{:S(2)}, u32[]{:S(2)}) collective-permute-start(f32[24,9,128]{2,1,0:T(8,128)S(1)} %get-tuple-element.7), channel_id=1, source_target_pairs={{18,0},{20,2},{22,4},{24,6},{26,8},{28,10},{30,12},{0,14},{2,16},{... | collective-permute-start | bytes 331784 | tf_op jit(solution)/shard_map/ppermute | solution.py:23
  41.3 19.1 %collective-permute-start.6 = (f32[24,9,128]{2,1,0:T(8,128)S(1)}, f32[24,9,128]{2,1,0:T(8,128)S(1)}, u32[]{:S(2)}, u32[]{:S(2)}) collective-permute-start(f32[24,9,128]{2,1,0:T(8,128)S(1)} %get-tuple-element.6), channel_id=1, source_target_pairs={{16,0},{18,2},{20,4},{22,6},{24,8},{26,10},{28,12},{30,14},{0,16},... | collective-permute-start | bytes 331784 | tf_op jit(solution)/shard_map/ppermute | solution.py:23
  43.5 19.1 %collective-permute-start.7 = (f32[24,9,128]{2,1,0:T(8,128)S(1)}, f32[24,9,128]{2,1,0:T(8,128)S(1)}, u32[]{:S(2)}, u32[]{:S(2)}) collective-permute-start(f32[24,9,128]{2,1,0:T(8,128)S(1)} %get-tuple-element.5), channel_id=1, source_target_pairs={{14,0},{16,2},{18,4},{20,6},{22,8},{24,10},{26,12},{28,14},{30,16}... | collective-permute-start | bytes 331784 | tf_op jit(solution)/shard_map/ppermute | solution.py:23
  50.1 12.7 %copy-start.2 = (f32[192,2]{1,0:T(8,128)S(1)}, f32[192,2]{1,0:T(8,128)}, u32[]{:S(2)}) copy-start(f32[192,2]{1,0:T(8,128)} %constant.37) | copy-start | bytes 4612
  64.6 13.8 %copy-start = (f32[64,128]{1,0:T(8,128)S(1)}, f32[64,128]{1,0:T(8,128)}, u32[]{:S(2)}) copy-start(f32[64,128]{1,0:T(8,128)} %param.13) | copy-start | bytes 98308
  64.6 17.2 %copy-start.1 = (f32[64,128]{1,0:T(8,128)S(1)}, f32[64,128]{1,0:T(8,128)}, u32[]{:S(2)}) copy-start(f32[64,128]{1,0:T(8,128)} %param.12) | copy-start | bytes 98308
  82.6 16.4 %collective-permute-start.8 = (f32[24,128]{1,0:T(8,128)S(1)}, f32[24,128]{1,0:T(8,128)S(1)}, u32[]{:S(2)}, u32[]{:S(2)}) collective-permute-start(f32[24,128]{1,0:T(8,128)S(1)} %get-tuple-element.20), channel_id=1, source_target_pairs={{18,0},{20,2},{22,4},{24,6},{26,8},{28,10},{30,12},{0,14},{2,16},{... | collective-permute-start | bytes 36872 | tf_op jit(solution)/shard_map/ppermute | solution.py:23
  86.7 16.6 %collective-permute-start.9 = (f32[24,128]{1,0:T(8,128)S(1)}, f32[24,128]{1,0:T(8,128)S(1)}, u32[]{:S(2)}, u32[]{:S(2)}) collective-permute-start(f32[24,128]{1,0:T(8,128)S(1)} %get-tuple-element.19), channel_id=1, source_target_pairs={{16,0},{18,2},{20,4},{22,6},{24,8},{26,10},{28,12},{30,14},{0,16},... | collective-permute-start | bytes 36872 | tf_op jit(solution)/shard_map/ppermute | solution.py:23
  95.7 9.5 %collective-permute-start.10 = (f32[24,128]{1,0:T(8,128)S(1)}, f32[24,128]{1,0:T(8,128)S(1)}, u32[]{:S(2)}, u32[]{:S(2)}) collective-permute-start(f32[24,128]{1,0:T(8,128)S(1)} %get-tuple-element.18), channel_id=1, source_target_pairs={{14,0},{16,2},{18,4},{20,6},{22,8},{24,10},{26,12},{28,14},{30,16}... | collective-permute-start | bytes 36872 | tf_op jit(solution)/shard_map/ppermute | solution.py:23
  95.7 9.5 %collective-permute-start.11 = (f32[24,128]{1,0:T(8,128)S(1)}, f32[24,128]{1,0:T(8,128)S(1)}, u32[]{:S(2)}, u32[]{:S(2)}) collective-permute-start(f32[24,128]{1,0:T(8,128)S(1)} %get-tuple-element.17), channel_id=1, source_target_pairs={{2,0},{4,2},{6,4},{8,6},{10,8},{12,10},{14,12},{16,14},{18,16},{20... | collective-permute-start | bytes 36872 | tf_op jit(solution)/shard_map/ppermute | solution.py:23
  99.0 7.4 %collective-permute-start.12 = (f32[24,128]{1,0:T(8,128)S(1)}, f32[24,128]{1,0:T(8,128)S(1)}, u32[]{:S(2)}, u32[]{:S(2)}) collective-permute-start(f32[24,128]{1,0:T(8,128)S(1)} %get-tuple-element.16), channel_id=1, source_target_pairs={{30,0},{0,2},{2,4},{4,6},{6,8},{8,10},{10,12},{12,14},{14,16},{16,... | collective-permute-start | bytes 36872 | tf_op jit(solution)/shard_map/ppermute | solution.py:23
  99.0 7.4 %collective-permute-start.13 = (f32[24,128]{1,0:T(8,128)S(1)}, f32[24,128]{1,0:T(8,128)S(1)}, u32[]{:S(2)}, u32[]{:S(2)}) collective-permute-start(f32[24,128]{1,0:T(8,128)S(1)} %get-tuple-element.15), channel_id=1, source_target_pairs={{18,0},{20,2},{22,4},{24,6},{26,8},{28,10},{30,12},{0,14},{2,16},{... | collective-permute-start | bytes 36872 | tf_op jit(solution)/shard_map/ppermute | solution.py:23
  103.3 4.6 %collective-permute-start.14 = (f32[24,128]{1,0:T(8,128)S(1)}, f32[24,128]{1,0:T(8,128)S(1)}, u32[]{:S(2)}, u32[]{:S(2)}) collective-permute-start(f32[24,128]{1,0:T(8,128)S(1)} %get-tuple-element.14), channel_id=1, source_target_pairs={{16,0},{18,2},{20,4},{22,6},{24,8},{26,10},{28,12},{30,14},{0,16},... | collective-permute-start | bytes 36872 | tf_op jit(solution)/shard_map/ppermute | solution.py:23
  105.2 5.5 %collective-permute-start.15 = (f32[24,128]{1,0:T(8,128)S(1)}, f32[24,128]{1,0:T(8,128)S(1)}, u32[]{:S(2)}, u32[]{:S(2)}) collective-permute-start(f32[24,128]{1,0:T(8,128)S(1)} %get-tuple-element.13), channel_id=1, source_target_pairs={{14,0},{16,2},{18,4},{20,6},{22,8},{24,10},{26,12},{28,14},{30,16}... | collective-permute-start | bytes 36872 | tf_op jit(solution)/shard_map/ppermute | solution.py:23
  135.8 2.2 %copy-start.3 = (s32[64]{0:T(128)S(1)}, s32[64]{0:T(128)}, u32[]{:S(2)}) copy-start(s32[64]{0:T(128)} %param.15) | copy-start | bytes 772
Sparse Core Ops, SparseCore 0:
  138.1 15.9 all-reduce.2

commit v2 on v1

--- a/solution.py
+++ b/solution.py
@@ -25,13 +25,25 @@
 
 def fetch_ghosts(own, send_rows):
     per_direction = send_rows.shape[1]
+    domains = lax.axis_size("dom")
     picked = jnp.take(own, send_rows.reshape(-1), axis=0, mode="clip")
     picked = picked.reshape((len(DIRECTIONS), per_direction) + own.shape[1:])
-    arrived = [
-        passed_along(picked[number], "dom", col_step * GY + row_step)
-        for number, (col_step, row_step) in enumerate(DIRECTIONS)
-    ]
+    groups = {}
+    for number, (col_step, row_step) in enumerate(DIRECTIONS):
+        groups.setdefault((col_step * GY + row_step) % domains, []).append(number)
+    arrived = [None] * len(DIRECTIONS)
+    for distance, members in groups.items():
+        payload = jnp.concatenate([picked[number] for number in members], axis=0)
+        payload = passed_along(payload, "dom", distance)
+        for place, number in enumerate(members):
+            arrived[number] = payload[place * per_direction:(place + 1) * per_direction]
     return jnp.concatenate(arrived, axis=0)
+
+
+def task_sum(partial):
+    if lax.axis_size("task") != 2:
+        return lax.psum(partial, "task")
+    return partial + lax.ppermute(partial, "task", [(0, 1), (1, 0)])
 
 
 def place_ghosts(ghost_feat, per_direction):
@@ -44,15 +56,19 @@
 
 
 def pick_tasks(task_lists, task_counts):
-    both_lists, both_counts = (
-        lax.all_gather(task_lists, "task", axis=1, tiled=True),
-        lax.all_gather(task_counts, "task", axis=1, tiled=True),
-    )
-    list_pair = both_lists[0]
-    count_pair = both_counts[0]
-    capacity = list_pair.shape[1]
+    mine = jnp.concatenate([task_lists[0, 0], task_counts[0]], axis=0)
+    member_rank = lax.axis_index("task")
+    if lax.axis_size("task") == 2:
+        theirs = lax.ppermute(mine, "task", [(0, 1), (1, 0)])
+        first = jnp.where(member_rank == 0, mine, theirs)
+        second = jnp.where(member_rank == 0, theirs, mine)
+    else:
+        both = lax.all_gather(mine, "task", axis=0, tiled=False)
+        first, second = both[0], both[1]
+    capacity = task_lists.shape[2]
+    list_pair = (first[:capacity], second[:capacity])
+    count_pair = (first[capacity], second[capacity])
     overall = count_pair[0] + count_pair[1]
-    member_rank = lax.axis_index("task")
     my_count = (overall + 1 - member_rank) // 2
     places = 2 * jnp.arange(capacity, dtype=jnp.int32) + member_rank
     first_pick = list_pair[0][jnp.clip(places, 0, capacity - 1)]
@@ -221,7 +237,7 @@
         density_kernel, my_list, my_count, all_feat, (own_count, SUB, block_width)
     )
     partial_rho = KERNEL_NORM / smoothing**3 * jnp.sum(partial_rho, axis=1)
-    rho_own = lax.psum(partial_rho, "task") + masses * KERNEL_NORM / smoothing**3
+    rho_own = task_sum(partial_rho) + masses * KERNEL_NORM / smoothing**3
     ghost_rho = fetch_ghosts(rho_own, send_rows)
     all_rho = jnp.concatenate([rho_own, ghost_rho], axis=0)
     force_feat = jnp.concatenate([all_feat, all_rho[:, None]], axis=1)
@@ -229,7 +245,7 @@
     partial_force = run_kernel(
         force_kernel, my_list, my_count, force_feat, (own_count, 4, SUB, block_width)
     )
-    forces = lax.psum(jnp.sum(partial_force, axis=2), "task")
+    forces = task_sum(jnp.sum(partial_force, axis=2))
     density = jnp.where(valid, rho_own, 0.0)
     acceleration = jnp.where(valid[:, None, :], -forces[:, 0:3], 0.0)
     energy_rate = jnp.where(valid, forces[:, 3], 0.0)

time: 165 us -> 134 us (0.81)
  between operations: 16.3 us -> 2.91 us
  starting transfers between devices: 45.9 us -> 33.9 us
  blocking collectives: 7.04 us -> 0 us
  waiting for transfers between devices: 34.6 us -> 36.8 us
    psum x1 -> x0, waiting for transfers between devices: 16 us -> none  [local(): forces = lax.psum(jnp.sum(partial_force, axis=2), 'task')]
    ppermute x16 -> x10, waiting for transfers between devices: 18.6 us -> 34.4 us  [passed_along(): return lax.ppermute(block, axis, route)]
    ppermute x16 -> x10, starting transfers between devices: 45.8 us -> 33.2 us  [passed_along(): return lax.ppermute(block, axis, route)]
    psum x1 -> x0, blocking collectives: 3.41 us -> none  [local(): lax.psum(partial_rho, 'task') + masses * KERNEL_NORM / smoothing ** 3]
    ppermute x0 -> x3, waiting for transfers between devices: none -> 2.45 us  [the longest x2 2.44 us: task_sum(): return partial + lax.ppermute(partial, 'task', [(0, 1), (1, 0)])]
    unnamed x1 -> x0, blocking collectives: 1.84 us -> none
    all_gather x1 -> x0, blocking collectives: 1.8 us -> none  [pick_tasks(): lax.all_gather(task_lists, 'task', axis=1, tiled=True)]
    unnamed x31 -> x24, local copies, waits for them, and re-layouts: 3.34 us -> 3.69 us
  transfers between devices with their start and end apart: 17 -> 13, of which waited for: 8 -> 6; matrix products, arithmetic and copies ran while one was open for 4% -> 8% of each run, Pallas kernels for 0% -> 0%
where the time goes in v2:
time: 134 us
  Pallas kernels  37 us (28%)
  waiting for transfers between devices  36.8 us (27%)
  starting transfers between devices  33.9 us (25%)
  other arithmetic  11.7 us (9%)
  local copies, waits for them, and re-layouts  11.5 us (9%)
  between operations  2.91 us (2%)
    pallas_call x2, Pallas kernels, run_kernel(): pl.pallas_call(kernel, out_shape=jax.ShapeDtypeStruct(out_shape, jnp.floa...  37 us
    ppermute x10, waiting for transfers between devices, passed_along(): return lax.ppermute(block, axis, route)  34.4 us
    ppermute x10, starting transfers between devices, passed_along(): return lax.ppermute(block, axis, route)  33.2 us
    unnamed x24, local copies, waits for them, and re-layouts  3.69 us
  transfers between devices with their start and end apart: 13, of which 6 were waited for; matrix products, arithmetic and copies ran while one was open for 8% of the time, Pallas kernels for 0%

profile of v2, /device:TPU:0, one launch (start us, length us, event | category | flops | bytes accessed | tf_op | source)
XLA Modules:
  0.0 133.9 jit_solution(167051628524937477)
XLA Ops:
  2.5 0.8 reshape.119
  3.2 0.8 fusion.3
  4.1 1.0 copy.19
  5.0 1.0 copy.20
  6.0 1.8 %concatenate.40 = f32[64,9,128]{2,1,0:T(8,128)S(1)} concatenate(f32[64,3,128]{2,1,0:T(4,128)S(1)} %copy.19, f32[64,3,128]{2,1,0:T(4,128)S(1)} %copy.20, f32[64,1,128]{2,1,0:T(1,128)S(1)} %bitcast.23, f32[64,1,128]{2,1,0:T(1,128)} %bitcast.21, f32[64,1,128]{2,1,0:T(1,128)} %bitcast.24), dimensions={1} | concatenate | bytes 589824 | tf_op jit(solution)/shard_map/concatenate | solution.py:228
  7.8 0.7 broadcast_select_fusion
  11.5 0.9 gather_fusion.2
  12.5 4.5 %collective-permute-start.1 = (f32[48,9,128]{2,1,0:T(8,128)S(1)}, f32[48,9,128]{2,1,0:T(8,128)S(1)}, u32[]{:S(2)}, u32[]{:S(2)}) collective-permute-start(f32[48,9,128]{2,1,0:T(8,128)S(1)} %pad_maximum_fusion.1), channel_id=1, source_target_pairs={{18,0},{20,2},{22,4},{24,6},{26,8},{28,10},{30,12},{0,14},{2,16},{... | collective-permute-start | bytes 663560 | tf_op jit(solution)/shard_map/ppermute | solution.py:23
  17.1 2.7 %collective-permute-start.2 = (f32[48,9,128]{2,1,0:T(8,128)S(1)}, f32[48,9,128]{2,1,0:T(8,128)S(1)}, u32[]{:S(2)}, u32[]{:S(2)}) collective-permute-start(f32[48,9,128]{2,1,0:T(8,128)S(1)} %pad_maximum_fusion.2), channel_id=1, source_target_pairs={{16,0},{18,2},{20,4},{22,6},{24,8},{26,10},{28,12},{30,14},{0,16},... | collective-permute-start | bytes 663560 | tf_op jit(solution)/shard_map/ppermute | solution.py:23
  20.2 3.2 %collective-permute-start.4 = (f32[24,9,128]{2,1,0:T(8,128)S(1)}, f32[24,9,128]{2,1,0:T(8,128)}, u32[]{:S(2)}, u32[]{:S(2)}) collective-permute-start(f32[24,9,128]{2,1,0:T(8,128)S(1)} %get-tuple-element.6), channel_id=1, source_target_pairs={{2,0},{4,2},{6,4},{8,6},{10,8},{12,10},{14,12},{16,14},{18,16},{20... | collective-permute-start | bytes 331784 | tf_op jit(solution)/shard_map/ppermute | solution.py:23
  23.4 1.2 gather_fusion
  24.6 1.2 gather_fusion.1
  25.9 1.2 compare_select_fusion.2.task_ref
  27.1 25.3 %collective-permute-done.1 = f32[48,9,128]{2,1,0:T(8,128)S(1)} collective-permute-done((f32[48,9,128]{2,1,0:T(8,128)S(1)}, f32[48,9,128]{2,1,0:T(8,128)S(1)}, u32[]{:S(2)}, u32[]{:S(2)}) %collective-permute-start.1) | collective-permute-done | bytes 221216 | tf_op jit(solution)/shard_map/ppermute | solution.py:23
  52.4 1.8 %collective-permute-done.2 = f32[48,9,128]{2,1,0:T(8,128)S(1)} collective-permute-done((f32[48,9,128]{2,1,0:T(8,128)S(1)}, f32[48,9,128]{2,1,0:T(8,128)S(1)}, u32[]{:S(2)}, u32[]{:S(2)}) %collective-permute-start.2) | collective-permute-done | bytes 221216 | tf_op jit(solution)/shard_map/ppermute | solution.py:23
  54.3 0.9 constant_dynamic-update-slice_fusion.1
  55.4 0.7 copy-done.2
  56.4 1.6 %maximum_maximum_fusion.feat_ref = f32[256,9,128]{2,1,0:T(8,128)} fusion(f32[192,7,128]{2,1,0:T(8,128)S(1)} %slice.183, f32[192,2,128]{2,1,0:T(2,128)S(1)} %slice_add_fusion, f32[64,9,128]{2,1,0:T(8,128)S(1)} %concatenate.40), kind=kLoop, calls=%fused_computation.4 | loop fusion | flops 589824 | bytes 2359296 | tf_op jit(solution)/shard_map/concatenate | solution.py:233
  58.0 13.0 %shard_map.121 = f32[64,8,128]{2,1,0:T(8,128)} custom-call(s32[128]{0:T(128)} %compare_select_fusion.2.task_ref, s32[1]{0:T(128)} %bitcast.6.count_ref, f32[256,9,128]{2,1,0:T(8,128)} %maximum_maximum_fusion.feat_ref), custom_call_target="tpu_custom_call" | custom-call | tf_op jit(solution)/shard_map/pallas_call | solution.py:205
  71.0 1.0 reduce_sum.18
  72.2 1.2 collective-permute-done.6
  73.4 0.7 gather_fusion.3
  74.1 13.8 %collective-permute-start.7 = (f32[48,128]{1,0:T(8,128)S(1)}, f32[48,128]{1,0:T(8,128)S(1)}, u32[]{:S(2)}, u32[]{:S(2)}) collective-permute-start(f32[48,128]{1,0:T(8,128)S(1)} %pad_maximum_fusion.4), channel_id=1, source_target_pairs={{18,0},{20,2},{22,4},{24,6},{26,8},{28,10},{30,12},{0,14},{2,16},{... | collective-permute-start | bytes 73736 | tf_op jit(solution)/shard_map/ppermute | solution.py:23
  88.0 5.2 %collective-permute-start.8 = (f32[48,128]{1,0:T(8,128)S(1)}, f32[48,128]{1,0:T(8,128)S(1)}, u32[]{:S(2)}, u32[]{:S(2)}) collective-permute-start(f32[48,128]{1,0:T(8,128)S(1)} %pad_maximum_fusion.5), channel_id=1, source_target_pairs={{16,0},{18,2},{20,4},{22,6},{24,8},{26,10},{28,12},{30,14},{0,16},... | collective-permute-start | bytes 73736 | tf_op jit(solution)/shard_map/ppermute | solution.py:23
  93.2 3.3 %collective-permute-start.10 = (f32[24,128]{1,0:T(8,128)S(1)}, f32[24,128]{1,0:T(8,128)S(1)}, u32[]{:S(2)}, u32[]{:S(2)}) collective-permute-start(f32[24,128]{1,0:T(8,128)S(1)} %get-tuple-element.14), channel_id=1, source_target_pairs={{2,0},{4,2},{6,4},{8,6},{10,8},{12,10},{14,12},{16,14},{18,16},{20... | collective-permute-start | bytes 36872 | tf_op jit(solution)/shard_map/ppermute | solution.py:23
  96.5 2.3 %collective-permute-done.9 = f32[48,128]{1,0:T(8,128)S(1)} collective-permute-done((f32[48,128]{1,0:T(8,128)S(1)}, f32[48,128]{1,0:T(8,128)S(1)}, u32[]{:S(2)}, u32[]{:S(2)}) %collective-permute-start.9) | collective-permute-done | bytes 24608 | tf_op jit(solution)/shard_map/ppermute | solution.py:23
  98.8 5.0 %collective-permute-done.11 = f32[24,128]{1,0:T(8,128)S(1)} collective-permute-done((f32[24,128]{1,0:T(8,128)S(1)}, f32[24,128]{1,0:T(8,128)S(1)}, u32[]{:S(2)}, u32[]{:S(2)}) %collective-permute-start.11) | collective-permute-done | bytes 12320 | tf_op jit(solution)/shard_map/ppermute | solution.py:23
  103.8 1.7 %pad_maximum_fusion.feat_ref = f32[256,10,128]{2,1,0:T(8,128)} fusion(f32[256,1,128]{2,1,0:T(1,128)S(1)} %bitcast.22, f32[192,7,128]{2,1,0:T(8,128)S(1)} %slice.183, f32[192,2,128]{2,1,0:T(2,128)S(1)} %slice_add_fusion, f32[64,9,128]{2,1,0:T(8,128)S(1)} %concatenate.40), kind=kLoop, calls=%fused_computation.5 | loop fusion | flops 983040 | bytes 2621440 | tf_op jit(solution)/shard_map/concatenate | solution.py:243
  105.6 24.0 %shard_map.122 = f32[64,4,8,128]{3,2,1,0:T(8,128)} custom-call(s32[128]{0:T(128)} %compare_select_fusion.2.task_ref, s32[1]{0:T(128)} %bitcast.6.count_ref, f32[256,10,128]{2,1,0:T(8,128)} %pad_maximum_fusion.feat_ref), custom_call_target="tpu_custom_call" | custom-call | tf_op jit(solution)/shard_map/pallas_call | solution.py:205
  129.6 1.5 %reduce_sum.19 = f32[64,4,128]{2,1,0:T(4,128)S(1)} reduce(f32[64,4,8,128]{3,2,1,0:T(8,128)} %shard_map.122, f32[]{:T(128)} %constant.32.clone.1), dimensions={2}, to_apply=%region_1.2 | reduce | flops 229376 | bytes 1179652 | tf_op jit(solution)/shard_map/reduce_sum | solution.py:248
  131.3 1.2 collective-permute-done.12
  132.5 0.7 fusion.1
  (61 shorter events, 4.9 us)
Async XLA Ops:
  1.9 5.8 %collective-permute-start = (s32[129]{0:T(256)S(1)}, s32[129]{0:T(256)S(1)}, u32[]{:S(2)}, u32[]{:S(2)}) collective-permute-start(s32[129]{0:T(256)S(1)} %pad_add_fusion), channel_id=1, source_target_pairs={{0,1},{1,0},{2,3},{3,2},{4,5},{5,4},{6,7},{7,6},{8,9},{9,8},{10,11... | collective-permute-start | bytes 1556 | tf_op jit(solution)/shard_map/ppermute | solution.py:62
  12.5 39.8 %collective-permute-start.1 = (f32[48,9,128]{2,1,0:T(8,128)S(1)}, f32[48,9,128]{2,1,0:T(8,128)S(1)}, u32[]{:S(2)}, u32[]{:S(2)}) collective-permute-start(f32[48,9,128]{2,1,0:T(8,128)S(1)} %pad_maximum_fusion.1), channel_id=1, source_target_pairs={{18,0},{20,2},{22,4},{24,6},{26,8},{28,10},{30,12},{0,14},{2,16},{... | collective-permute-start | bytes 663560 | tf_op jit(solution)/shard_map/ppermute | solution.py:23
  17.1 37.1 %collective-permute-start.2 = (f32[48,9,128]{2,1,0:T(8,128)S(1)}, f32[48,9,128]{2,1,0:T(8,128)S(1)}, u32[]{:S(2)}, u32[]{:S(2)}) collective-permute-start(f32[48,9,128]{2,1,0:T(8,128)S(1)} %pad_maximum_fusion.2), channel_id=1, source_target_pairs={{16,0},{18,2},{20,4},{22,6},{24,8},{26,10},{28,12},{30,14},{0,16},... | collective-permute-start | bytes 663560 | tf_op jit(solution)/shard_map/ppermute | solution.py:23
  19.8 34.5 %collective-permute-start.3 = (f32[48,9,128]{2,1,0:T(8,128)S(1)}, f32[48,9,128]{2,1,0:T(8,128)S(1)}, u32[]{:S(2)}, u32[]{:S(2)}) collective-permute-start(f32[48,9,128]{2,1,0:T(8,128)S(1)} %pad_maximum_fusion.3), channel_id=1, source_target_pairs={{14,0},{16,2},{18,4},{20,6},{22,8},{24,10},{26,12},{28,14},{30,16}... | collective-permute-start | bytes 663560 | tf_op jit(solution)/shard_map/ppermute | solution.py:23
  20.2 34.1 %collective-permute-start.4 = (f32[24,9,128]{2,1,0:T(8,128)S(1)}, f32[24,9,128]{2,1,0:T(8,128)}, u32[]{:S(2)}, u32[]{:S(2)}) collective-permute-start(f32[24,9,128]{2,1,0:T(8,128)S(1)} %get-tuple-element.6), channel_id=1, source_target_pairs={{2,0},{4,2},{6,4},{8,6},{10,8},{12,10},{14,12},{16,14},{18,16},{20... | collective-permute-start | bytes 331784 | tf_op jit(solution)/shard_map/ppermute | solution.py:23
  23.4 31.8 %collective-permute-start.5 = (f32[24,9,128]{2,1,0:T(8,128)S(1)}, f32[24,9,128]{2,1,0:T(8,128)S(1)}, u32[]{:S(2)}, u32[]{:S(2)}) collective-permute-start(f32[24,9,128]{2,1,0:T(8,128)S(1)} %get-tuple-element.5), channel_id=1, source_target_pairs={{30,0},{0,2},{2,4},{4,6},{6,8},{8,10},{10,12},{12,14},{14,16},{16,... | collective-permute-start | bytes 331784 | tf_op jit(solution)/shard_map/ppermute | solution.py:23
  55.2 0.9 copy-start.2
  58.0 14.1 %copy-start = (f32[64,128]{1,0:T(8,128)S(1)}, f32[64,128]{1,0:T(8,128)}, u32[]{:S(2)}) copy-start(f32[64,128]{1,0:T(8,128)} %param.13) | copy-start | bytes 98308
  58.0 15.4 %copy-start.1 = (f32[64,128]{1,0:T(8,128)S(1)}, f32[64,128]{1,0:T(8,128)}, u32[]{:S(2)}) copy-start(f32[64,128]{1,0:T(8,128)} %param.12) | copy-start | bytes 98308
  72.1 1.3 collective-permute-start.6
  74.1 22.4 %collective-permute-start.7 = (f32[48,128]{1,0:T(8,128)S(1)}, f32[48,128]{1,0:T(8,128)S(1)}, u32[]{:S(2)}, u32[]{:S(2)}) collective-permute-start(f32[48,128]{1,0:T(8,128)S(1)} %pad_maximum_fusion.4), channel_id=1, source_target_pairs={{18,0},{20,2},{22,4},{24,6},{26,8},{28,10},{30,12},{0,14},{2,16},{... | collective-permute-start | bytes 73736 | tf_op jit(solution)/shard_map/ppermute | solution.py:23
  88.0 8.6 %collective-permute-start.8 = (f32[48,128]{1,0:T(8,128)S(1)}, f32[48,128]{1,0:T(8,128)S(1)}, u32[]{:S(2)}, u32[]{:S(2)}) collective-permute-start(f32[48,128]{1,0:T(8,128)S(1)} %pad_maximum_fusion.5), channel_id=1, source_target_pairs={{16,0},{18,2},{20,4},{22,6},{24,8},{26,10},{28,12},{30,14},{0,16},... | collective-permute-start | bytes 73736 | tf_op jit(solution)/shard_map/ppermute | solution.py:23
  93.2 5.6 %collective-permute-start.9 = (f32[48,128]{1,0:T(8,128)S(1)}, f32[48,128]{1,0:T(8,128)S(1)}, u32[]{:S(2)}, u32[]{:S(2)}) collective-permute-start(f32[48,128]{1,0:T(8,128)S(1)} %pad_maximum_fusion.6), channel_id=1, source_target_pairs={{14,0},{16,2},{18,4},{20,6},{22,8},{24,10},{26,12},{28,14},{30,16}... | collective-permute-start | bytes 73736 | tf_op jit(solution)/shard_map/ppermute | solution.py:23
  93.2 5.6 %collective-permute-start.10 = (f32[24,128]{1,0:T(8,128)S(1)}, f32[24,128]{1,0:T(8,128)S(1)}, u32[]{:S(2)}, u32[]{:S(2)}) collective-permute-start(f32[24,128]{1,0:T(8,128)S(1)} %get-tuple-element.14), channel_id=1, source_target_pairs={{2,0},{4,2},{6,4},{8,6},{10,8},{12,10},{14,12},{16,14},{18,16},{20... | collective-permute-start | bytes 36872 | tf_op jit(solution)/shard_map/ppermute | solution.py:23
  96.5 7.3 %collective-permute-start.11 = (f32[24,128]{1,0:T(8,128)S(1)}, f32[24,128]{1,0:T(8,128)S(1)}, u32[]{:S(2)}, u32[]{:S(2)}) collective-permute-start(f32[24,128]{1,0:T(8,128)S(1)} %get-tuple-element.13), channel_id=1, source_target_pairs={{30,0},{0,2},{2,4},{4,6},{6,8},{8,10},{10,12},{12,14},{14,16},{16,... | collective-permute-start | bytes 36872 | tf_op jit(solution)/shard_map/ppermute | solution.py:23
  105.6 25.6 %copy-start.3 = (s32[64]{0:T(128)S(1)}, s32[64]{0:T(128)}, u32[]{:S(2)}) copy-start(s32[64]{0:T(128)} %param.15) | copy-start | bytes 772
  131.1 1.4 %collective-permute-start.12 = (f32[64,4,128]{2,0,1:T(8,128)S(1)}, f32[64,4,128]{2,0,1:T(8,128)S(1)}, u32[]{:S(2)}, u32[]{:S(2)}) collective-permute-start(f32[64,4,128]{2,0,1:T(8,128)S(1)} %copy.23), channel_id=1, source_target_pairs={{0,1},{1,0},{2,3},{3,2},{4,5},{5,4},{6,7},{7,6},{8,9},{9,8},{10,11... | collective-permute-start | bytes 393224 | tf_op jit(solution)/shard_map/ppermute | solution.py:46

commit v3 on v2

--- a/solution.py
+++ b/solution.py
@@ -6,6 +6,7 @@
 from jax.experimental import pallas as pl
 from jax.experimental.pallas import tpu as pltpu
 from jax.sharding import PartitionSpec as P
+
 
 GY = 8
 
@@ -100,11 +101,11 @@
         xi = spread(tb[0:1])
         yi = spread(tb[1:2])
         zi = spread(tb[2:3])
-        hinv = spread(1.0 / tb[7:8])
+        hinv = spread(1.0 / tb[4:5])
         xs = spread(sb[0:1])
         ys = spread(sb[1:2])
         zs = spread(sb[2:3])
-        ms = spread(sb[6:7])
+        ms = spread(sb[3:4])
         acc = jnp.zeros((SUB, lanes), jnp.float32)
         for tile in range(lanes // SUB):
             dx = xi - turned(xs, tile)
@@ -199,18 +200,22 @@
     lax.fori_loop(0, count_ref[0], one_task, 0)
 
 
-def run_kernel(kernel, my_list, my_count, feat, out_shape):
+def run_kernel(kernel, my_list, my_count, feat, out_shape, pair_cost):
     smem = pl.BlockSpec(memory_space=pltpu.SMEM)
     vmem = pl.BlockSpec(memory_space=pltpu.VMEM)
+    pairs = my_list.shape[0] * feat.shape[2] * feat.shape[2]
     return pl.pallas_call(
         kernel,
         out_shape=jax.ShapeDtypeStruct(out_shape, jnp.float32),
         in_specs=[smem, smem, vmem],
         out_specs=vmem,
+        cost_estimate=pl.CostEstimate(
+            flops=pairs * pair_cost, transcendentals=pairs, bytes_accessed=feat.size * 4
+        ),
     )(my_list, jnp.reshape(my_count, (1,)).astype(jnp.int32), feat)
 
 
-def local(
+def local_body(
     positions,
     velocities,
     masses,
@@ -225,25 +230,31 @@
     block_width = positions.shape[2]
     valid = jnp.arange(block_width, dtype=jnp.int32)[None, :] < block_counts[:, None]
     live_mass = jnp.where(valid, masses, 0.0)
-    own_feat = jnp.concatenate(
-        [positions, velocities, live_mass[:, None], smoothing[:, None], energy[:, None]], axis=1
-    )
     send_rows = send_lists[0]
-    ghost_feat = place_ghosts(fetch_ghosts(own_feat, send_rows), send_rows.shape[1])
-    all_feat = jnp.concatenate([own_feat, ghost_feat], axis=0)
+    per_direction = send_rows.shape[1]
+    own_near = jnp.concatenate([positions, live_mass[:, None], smoothing[:, None]], axis=1)
+    own_move = jnp.concatenate([velocities, energy[:, None]], axis=1)
+    ghost_near = place_ghosts(fetch_ghosts(own_near, send_rows), per_direction)
+    own_move, ghost_near = lax.optimization_barrier((own_move, ghost_near))
+    ghost_move = fetch_ghosts(own_move, send_rows)
+    all_near = jnp.concatenate([own_near, ghost_near], axis=0)
     my_list, my_count = pick_tasks(task_lists, task_counts)
 
     partial_rho = run_kernel(
-        density_kernel, my_list, my_count, all_feat, (own_count, SUB, block_width)
+        density_kernel, my_list, my_count, all_near, (own_count, SUB, block_width), 4096
     )
     partial_rho = KERNEL_NORM / smoothing**3 * jnp.sum(partial_rho, axis=1)
     rho_own = task_sum(partial_rho) + masses * KERNEL_NORM / smoothing**3
     ghost_rho = fetch_ghosts(rho_own, send_rows)
     all_rho = jnp.concatenate([rho_own, ghost_rho], axis=0)
-    force_feat = jnp.concatenate([all_feat, all_rho[:, None]], axis=1)
+    all_move = jnp.concatenate([own_move, ghost_move], axis=0)
+    force_feat = jnp.concatenate(
+        [all_near[:, 0:3], all_move[:, 0:3], all_near[:, 3:5], all_move[:, 3:4], all_rho[:, None]],
+        axis=1,
+    )
 
     partial_force = run_kernel(
-        force_kernel, my_list, my_count, force_feat, (own_count, 4, SUB, block_width)
+        force_kernel, my_list, my_count, force_feat, (own_count, 4, SUB, block_width), 8192
     )
     forces = task_sum(jnp.sum(partial_force, axis=2))
     density = jnp.where(valid, rho_own, 0.0)
@@ -265,7 +276,7 @@
         P("dom", "task"),
     )
     return jax.shard_map(
-        local,
+        local_body,
         mesh=mesh,
         in_specs=placed,
         out_specs=(P("dom", None), P("dom", None, None), P("dom", None)),

time: 134 us -> 139 us (1.037)
  waiting for transfers between devices: 36.8 us -> 46.6 us
  starting transfers between devices: 33.9 us -> 28.6 us
  local copies, waits for them, and re-layouts: 11.5 us -> 13.9 us
    ppermute x10 -> x15, waiting for transfers between devices: 34.4 us -> 45.3 us  [passed_along(): return lax.ppermute(block, axis, route)]
    ppermute x10 -> x15, starting transfers between devices: 33.2 us -> 27.9 us  [passed_along(): return lax.ppermute(block, axis, route)]
    concatenate x2 -> x3, local copies, waits for them, and re-layouts: 1.77 us -> 3.66 us  [the longest x1 3.65 us: local_body(): jnp.concatenate([all_near[:, 0:3], all_move[:, 0:3], all_near[:, 3:5], al...]
    concatenate x2 -> x4, other arithmetic: 3.36 us -> 1.99 us  [the longest x1 0.85 us: local_body(): jnp.concatenate([positions, live_mass[:, None], smoothing[:, None]], axis=1)]
    unnamed x24 -> x34, local copies, waits for them, and re-layouts: 3.69 us -> 2.98 us
  transfers between devices with their start and end apart: 13 -> 18, of which waited for: 6 -> 8; matrix products, arithmetic and copies ran while one was open for 8% -> 7% of each run, Pallas kernels for 0% -> 0%
where the time goes in v3:
time: 139 us
  waiting for transfers between devices  46.6 us (34%)
  Pallas kernels  36.2 us (26%)
  starting transfers between devices  28.6 us (21%)
  local copies, waits for them, and re-layouts  13.9 us (10%)
  other arithmetic  10.4 us (7%)
  between operations  3.1 us (2%)
    ppermute x15, waiting for transfers between devices, passed_along(): return lax.ppermute(block, axis, route)  45.3 us
    pallas_call x2, Pallas kernels, run_kernel(): pl.pallas_call(kernel, out_shape=jax.ShapeDtypeStruct(out_shape, jnp.floa...  36.2 us
    ppermute x15, starting transfers between devices, passed_along(): return lax.ppermute(block, axis, route)  27.9 us
    concatenate x1, local copies, waits for them, and re-layouts, local_body(): jnp.concatenate([all_near[:, 0:3], all_move[:, 0:3], all_near[:, 3:5], al...  3.65 us
    unnamed x34, local copies, waits for them, and re-layouts  2.98 us
  transfers between devices with their start and end apart: 18, of which 8 were waited for; matrix products, arithmetic and copies ran while one was open for 7% of the time, Pallas kernels for 0%

profile of v3, /device:TPU:0, one launch (start us, length us, event | category | flops | bytes accessed | tf_op | source)
XLA Modules:
  0.0 138.8 jit_solution(17996879011843946244)
XLA Ops:
  2.4 1.0 copy.19
  3.4 1.0 copy.21
  6.0 0.8 pad_maximum_fusion.2
  11.4 0.9 gather_fusion.2
  12.4 3.6 %collective-permute-start.2 = (f32[48,5,128]{2,1,0:T(8,128)S(1)}, f32[48,5,128]{2,1,0:T(8,128)S(1)}, u32[]{:S(2)}, u32[]{:S(2)}) collective-permute-start(f32[48,5,128]{2,1,0:T(8,128)S(1)} %pad_maximum_fusion.4), channel_id=1, source_target_pairs={{16,0},{18,2},{20,4},{22,6},{24,8},{26,10},{28,12},{30,14},{0,16},... | collective-permute-start | bytes 368648 | tf_op jit(solution)/shard_map/ppermute | solution.py:24
  16.1 3.5 %collective-permute-start.1 = (f32[48,5,128]{2,1,0:T(8,128)S(1)}, f32[48,5,128]{2,1,0:T(8,128)S(1)}, u32[]{:S(2)}, u32[]{:S(2)}) collective-permute-start(f32[48,5,128]{2,1,0:T(8,128)S(1)} %pad_maximum_fusion.3), channel_id=1, source_target_pairs={{18,0},{20,2},{22,4},{24,6},{26,8},{28,10},{30,12},{0,14},{2,16},{... | collective-permute-start | bytes 368648 | tf_op jit(solution)/shard_map/ppermute | solution.py:24
  20.0 3.2 %collective-permute-start.4 = (f32[24,5,128]{2,1,0:T(8,128)S(1)}, f32[24,5,128]{2,1,0:T(8,128)S(1)}, u32[]{:S(2)}, u32[]{:S(2)}) collective-permute-start(f32[24,5,128]{2,1,0:T(8,128)S(1)} %get-tuple-element.10), channel_id=1, source_target_pairs={{2,0},{4,2},{6,4},{8,6},{10,8},{12,10},{14,12},{16,14},{18,16},{20... | collective-permute-start | bytes 184328 | tf_op jit(solution)/shard_map/ppermute | solution.py:24
  23.2 1.2 gather_fusion.1
  24.5 1.2 gather_fusion
  25.7 1.2 compare_select_fusion.2.task_ref
  26.9 13.0 %collective-permute-done.1 = f32[48,5,128]{2,1,0:T(8,128)S(1)} collective-permute-done((f32[48,5,128]{2,1,0:T(8,128)S(1)}, f32[48,5,128]{2,1,0:T(8,128)S(1)}, u32[]{:S(2)}, u32[]{:S(2)}) %collective-permute-start.1) | collective-permute-done | bytes 122912 | tf_op jit(solution)/shard_map/ppermute | solution.py:24
  40.6 0.9 gather_fusion.3
  41.9 0.9 copy-done
  42.7 12.5 %shard_map.121 = f32[64,8,128]{2,1,0:T(8,128)} custom-call(s32[128]{0:T(128)} %compare_select_fusion.2.task_ref, s32[1]{0:T(128)} %bitcast.6.count_ref, f32[256,5,128]{2,1,0:T(8,128)} %copy-done), custom_call_target="tpu_custom_call" | custom-call | flops 8589934592 | bytes 655360 | tf_op jit(solution)/shard_map/pallas_call | solution.py:207
  55.2 1.0 reduce_sum.18
  56.4 1.8 %collective-permute-start.9 = (f32[48,4,128]{2,1,0:T(4,128)S(1)}, f32[48,4,128]{2,1,0:T(4,128)S(1)}, u32[]{:S(2)}, u32[]{:S(2)}) collective-permute-start(f32[48,4,128]{2,1,0:T(4,128)S(1)} %pad_maximum_fusion.9), channel_id=1, source_target_pairs={{14,0},{16,2},{18,4},{20,6},{22,8},{24,10},{26,12},{28,14},{30,16}... | collective-permute-start | bytes 294920 | tf_op jit(solution)/shard_map/ppermute | solution.py:24
  58.3 2.3 %collective-permute-start.8 = (f32[48,4,128]{2,1,0:T(4,128)S(1)}, f32[48,4,128]{2,1,0:T(4,128)S(1)}, u32[]{:S(2)}, u32[]{:S(2)}) collective-permute-start(f32[48,4,128]{2,1,0:T(4,128)S(1)} %pad_maximum_fusion.8), channel_id=1, source_target_pairs={{16,0},{18,2},{20,4},{22,6},{24,8},{26,10},{28,12},{30,14},{0,16},... | collective-permute-start | bytes 294920 | tf_op jit(solution)/shard_map/ppermute | solution.py:24
  60.6 3.9 %collective-permute-start.7 = (f32[48,4,128]{2,1,0:T(4,128)S(1)}, f32[48,4,128]{2,1,0:T(4,128)S(1)}, u32[]{:S(2)}, u32[]{:S(2)}) collective-permute-start(f32[48,4,128]{2,1,0:T(4,128)S(1)} %pad_maximum_fusion.7), channel_id=1, source_target_pairs={{18,0},{20,2},{22,4},{24,6},{26,8},{28,10},{30,12},{0,14},{2,16},{... | collective-permute-start | bytes 294920 | tf_op jit(solution)/shard_map/ppermute | solution.py:24
  64.4 2.4 %collective-permute-start.10 = (f32[24,4,128]{2,1,0:T(4,128)S(1)}, f32[24,4,128]{2,1,0:T(4,128)S(1)}, u32[]{:S(2)}, u32[]{:S(2)}) collective-permute-start(f32[24,4,128]{2,1,0:T(4,128)S(1)} %get-tuple-element.18), channel_id=1, source_target_pairs={{2,0},{4,2},{6,4},{8,6},{10,8},{12,10},{14,12},{16,14},{18,16},{20... | collective-permute-start | bytes 147464 | tf_op jit(solution)/shard_map/ppermute | solution.py:24
  67.6 3.0 %collective-permute-start.12 = (f32[48,128]{1,0:T(8,128)S(1)}, f32[48,128]{1,0:T(8,128)S(1)}, u32[]{:S(2)}, u32[]{:S(2)}) collective-permute-start(f32[48,128]{1,0:T(8,128)S(1)} %pad_maximum_fusion.10), channel_id=1, source_target_pairs={{18,0},{20,2},{22,4},{24,6},{26,8},{28,10},{30,12},{0,14},{2,16},{... | collective-permute-start | bytes 73736 | tf_op jit(solution)/shard_map/ppermute | solution.py:24
  70.6 7.2 %collective-permute-done.12 = f32[48,128]{1,0:T(8,128)S(1)} collective-permute-done((f32[48,128]{1,0:T(8,128)S(1)}, f32[48,128]{1,0:T(8,128)S(1)}, u32[]{:S(2)}, u32[]{:S(2)}) %collective-permute-start.12) | collective-permute-done | bytes 24608 | tf_op jit(solution)/shard_map/ppermute | solution.py:24
  77.7 4.7 %collective-permute-done.13 = f32[48,128]{1,0:T(8,128)S(1)} collective-permute-done((f32[48,128]{1,0:T(8,128)S(1)}, f32[48,128]{1,0:T(8,128)S(1)}, u32[]{:S(2)}, u32[]{:S(2)}) %collective-permute-start.13) | collective-permute-done | bytes 24608 | tf_op jit(solution)/shard_map/ppermute | solution.py:24
  82.5 1.0 collective-permute-start.14
  83.5 4.6 %collective-permute-done.14 = f32[48,128]{1,0:T(8,128)S(1)} collective-permute-done((f32[48,128]{1,0:T(8,128)S(1)}, f32[48,128]{1,0:T(8,128)S(1)}, u32[]{:S(2)}, u32[]{:S(2)}) %collective-permute-start.14) | collective-permute-done | bytes 24608 | tf_op jit(solution)/shard_map/ppermute | solution.py:24
  88.1 3.8 %collective-permute-done.15 = f32[24,128]{1,0:T(8,128)S(1)} collective-permute-done((f32[24,128]{1,0:T(8,128)S(1)}, f32[24,128]{1,0:T(8,128)S(1)}, u32[]{:S(2)}, u32[]{:S(2)}) %collective-permute-start.15) | collective-permute-done | bytes 12320 | tf_op jit(solution)/shard_map/ppermute | solution.py:24
  91.9 2.8 %collective-permute-start.16 = (f32[24,128]{1,0:T(8,128)S(1)}, f32[24,128]{1,0:T(8,128)S(1)}, u32[]{:S(2)}, u32[]{:S(2)}) collective-permute-start(f32[24,128]{1,0:T(8,128)S(1)} %get-tuple-element.25), channel_id=1, source_target_pairs={{30,0},{0,2},{2,4},{4,6},{6,8},{8,10},{10,12},{12,14},{14,16},{16,... | collective-permute-start | bytes 36872 | tf_op jit(solution)/shard_map/ppermute | solution.py:24
  94.7 4.5 %collective-permute-done.16 = f32[24,128]{1,0:T(8,128)S(1)} collective-permute-done((f32[24,128]{1,0:T(8,128)S(1)}, f32[24,128]{1,0:T(8,128)S(1)}, u32[]{:S(2)}, u32[]{:S(2)}) %collective-permute-start.16) | collective-permute-done | bytes 12320 | tf_op jit(solution)/shard_map/ppermute | solution.py:24
  99.3 7.5 %collective-permute-done.11 = f32[24,4,128]{2,1,0:T(4,128)S(1)} collective-permute-done((f32[24,4,128]{2,1,0:T(4,128)S(1)}, f32[24,4,128]{2,1,0:T(4,128)S(1)}, u32[]{:S(2)}, u32[]{:S(2)}) %collective-permute-start.11) | collective-permute-done | bytes 49184 | tf_op jit(solution)/shard_map/ppermute | solution.py:24
  107.0 3.6 %concatenate.71.feat_ref = f32[256,10,128]{2,1,0:T(8,128)} concatenate(f32[256,3,128]{2,1,0:T(4,128)S(1)} %slice-done, f32[256,3,128]{2,1,0:T(4,128)S(1)} %bitcast.22, f32[256,2,128]{2,1,0:T(2,128)S(1)} %slice.282, f32[256,1,128]{2,1,0:T(1,128)S(1)} %slice.283, f32[256,1,128]{2,1,0:T(1,128)S(1)} %bitcast.27), dimensions={1} | concatenate | bytes 2621440 | tf_op jit(solution)/shard_map/concatenate | solution.py:251
  110.7 23.7 %shard_map.122 = f32[64,4,8,128]{3,2,1,0:T(8,128)} custom-call(s32[128]{0:T(128)} %compare_select_fusion.2.task_ref, s32[1]{0:T(128)} %bitcast.6.count_ref, f32[256,10,128]{2,1,0:T(8,128)} %concatenate.71.feat_ref), custom_call_target="tpu_custom_call" | custom-call | flops 17179869184 | bytes 1310720 | tf_op jit(solution)/shard_map/pallas_call | solution.py:207
  134.4 1.5 %reduce_sum.19 = f32[64,4,128]{2,1,0:T(4,128)S(1)} reduce(f32[64,4,8,128]{3,2,1,0:T(8,128)} %shard_map.122, f32[]{:T(128)} %constant.32.clone.1), dimensions={2}, to_apply=%region_1.2 | reduce | flops 229376 | bytes 1179652 | tf_op jit(solution)/shard_map/reduce_sum | solution.py:259
  136.1 1.2 collective-permute-done.17
  (93 shorter events, 10.2 us)
Async XLA Ops:
  1.9 5.7 %collective-permute-start = (s32[129]{0:T(256)S(1)}, s32[129]{0:T(256)S(1)}, u32[]{:S(2)}, u32[]{:S(2)}) collective-permute-start(s32[129]{0:T(256)S(1)} %pad_add_fusion), channel_id=1, source_target_pairs={{0,1},{1,0},{2,3},{3,2},{4,5},{5,4},{6,7},{7,6},{8,9},{9,8},{10,11... | collective-permute-start | bytes 1556 | tf_op jit(solution)/shard_map/ppermute | solution.py:63
  12.4 27.5 %collective-permute-start.2 = (f32[48,5,128]{2,1,0:T(8,128)S(1)}, f32[48,5,128]{2,1,0:T(8,128)S(1)}, u32[]{:S(2)}, u32[]{:S(2)}) collective-permute-start(f32[48,5,128]{2,1,0:T(8,128)S(1)} %pad_maximum_fusion.4), channel_id=1, source_target_pairs={{16,0},{18,2},{20,4},{22,6},{24,8},{26,10},{28,12},{30,14},{0,16},... | collective-permute-start | bytes 368648 | tf_op jit(solution)/shard_map/ppermute | solution.py:24
  16.0 24.2 %copy-start.3 = (f32[192,2]{1,0:T(8,128)S(1)}, f32[192,2]{1,0:T(8,128)}, u32[]{:S(2)}) copy-start(f32[192,2]{1,0:T(8,128)} %constant.37) | copy-start | bytes 4612
  16.1 23.8 %collective-permute-start.1 = (f32[48,5,128]{2,1,0:T(8,128)S(1)}, f32[48,5,128]{2,1,0:T(8,128)S(1)}, u32[]{:S(2)}, u32[]{:S(2)}) collective-permute-start(f32[48,5,128]{2,1,0:T(8,128)S(1)} %pad_maximum_fusion.3), channel_id=1, source_target_pairs={{18,0},{20,2},{22,4},{24,6},{26,8},{28,10},{30,12},{0,14},{2,16},{... | collective-permute-start | bytes 368648 | tf_op jit(solution)/shard_map/ppermute | solution.py:24
  19.6 20.3 %collective-permute-start.3 = (f32[48,5,128]{2,1,0:T(8,128)S(1)}, f32[48,5,128]{2,1,0:T(8,128)S(1)}, u32[]{:S(2)}, u32[]{:S(2)}) collective-permute-start(f32[48,5,128]{2,1,0:T(8,128)S(1)} %pad_maximum_fusion.5), channel_id=1, source_target_pairs={{14,0},{16,2},{18,4},{20,6},{22,8},{24,10},{26,12},{28,14},{30,16}... | collective-permute-start | bytes 368648 | tf_op jit(solution)/shard_map/ppermute | solution.py:24
  20.0 20.0 %collective-permute-start.4 = (f32[24,5,128]{2,1,0:T(8,128)S(1)}, f32[24,5,128]{2,1,0:T(8,128)S(1)}, u32[]{:S(2)}, u32[]{:S(2)}) collective-permute-start(f32[24,5,128]{2,1,0:T(8,128)S(1)} %get-tuple-element.10), channel_id=1, source_target_pairs={{2,0},{4,2},{6,4},{8,6},{10,8},{12,10},{14,12},{16,14},{18,16},{20... | collective-permute-start | bytes 184328 | tf_op jit(solution)/shard_map/ppermute | solution.py:24
  23.2 16.8 %collective-permute-start.5 = (f32[24,5,128]{2,1,0:T(8,128)S(1)}, f32[24,5,128]{2,1,0:T(8,128)S(1)}, u32[]{:S(2)}, u32[]{:S(2)}) collective-permute-start(f32[24,5,128]{2,1,0:T(8,128)S(1)} %get-tuple-element.9), channel_id=1, source_target_pairs={{30,0},{0,2},{2,4},{4,6},{6,8},{8,10},{10,12},{12,14},{14,16},{16,... | collective-permute-start | bytes 184328 | tf_op jit(solution)/shard_map/ppermute | solution.py:24
  40.0 1.5 %copy-start.1 = (f32[64,128]{1,0:T(8,128)S(1)}, f32[64,128]{1,0:T(8,128)}, u32[]{:S(2)}) copy-start(f32[64,128]{1,0:T(8,128)} %param.13) | copy-start | bytes 98308
  41.7 1.0 copy-start
  42.7 24.1 %copy-start.2 = (f32[64,128]{1,0:T(8,128)S(1)}, f32[64,128]{1,0:T(8,128)}, u32[]{:S(2)}) copy-start(f32[64,128]{1,0:T(8,128)} %param.12) | copy-start | bytes 98308
  56.3 50.8 %slice-start = ((f32[256,5,128]{2,1,0:T(8,128)}), f32[256,3,128]{2,1,0:T(4,128)S(1)}, s32[]{:S(2)}) async-start(f32[256,5,128]{2,1,0:T(8,128)} %copy-done), calls=%async_computation | async-start | bytes 1048576 | tf_op jit(solution)/shard_map/slice | solution.py:252
  56.3 10.6 %collective-permute-start.6 = (f32[64,128]{1,0:T(8,128)S(1)}, f32[64,128]{1,0:T(8,128)S(1)}, u32[]{:S(2)}, u32[]{:S(2)}) collective-permute-start(f32[64,128]{1,0:T(8,128)S(1)} %divide_multiply_fusion), channel_id=1, source_target_pairs={{0,1},{1,0},{2,3},{3,2},{4,5},{5,4},{6,7},{7,6},{8,9},{9,8},{10,11... | collective-permute-start | bytes 98312 | tf_op jit(solution)/shard_map/ppermute | solution.py:47
  56.4 42.8 %collective-permute-start.9 = (f32[48,4,128]{2,1,0:T(4,128)S(1)}, f32[48,4,128]{2,1,0:T(4,128)S(1)}, u32[]{:S(2)}, u32[]{:S(2)}) collective-permute-start(f32[48,4,128]{2,1,0:T(4,128)S(1)} %pad_maximum_fusion.9), channel_id=1, source_target_pairs={{14,0},{16,2},{18,4},{20,6},{22,8},{24,10},{26,12},{28,14},{30,16}... | collective-permute-start | bytes 294920 | tf_op jit(solution)/shard_map/ppermute | solution.py:24
  58.3 40.9 %collective-permute-start.8 = (f32[48,4,128]{2,1,0:T(4,128)S(1)}, f32[48,4,128]{2,1,0:T(4,128)S(1)}, u32[]{:S(2)}, u32[]{:S(2)}) collective-permute-start(f32[48,4,128]{2,1,0:T(4,128)S(1)} %pad_maximum_fusion.8), channel_id=1, source_target_pairs={{16,0},{18,2},{20,4},{22,6},{24,8},{26,10},{28,12},{30,14},{0,16},... | collective-permute-start | bytes 294920 | tf_op jit(solution)/shard_map/ppermute | solution.py:24
  60.6 38.6 %collective-permute-start.7 = (f32[48,4,128]{2,1,0:T(4,128)S(1)}, f32[48,4,128]{2,1,0:T(4,128)S(1)}, u32[]{:S(2)}, u32[]{:S(2)}) collective-permute-start(f32[48,4,128]{2,1,0:T(4,128)S(1)} %pad_maximum_fusion.7), channel_id=1, source_target_pairs={{18,0},{20,2},{22,4},{24,6},{26,8},{28,10},{30,12},{0,14},{2,16},{... | collective-permute-start | bytes 294920 | tf_op jit(solution)/shard_map/ppermute | solution.py:24
  64.4 34.8 %collective-permute-start.10 = (f32[24,4,128]{2,1,0:T(4,128)S(1)}, f32[24,4,128]{2,1,0:T(4,128)S(1)}, u32[]{:S(2)}, u32[]{:S(2)}) collective-permute-start(f32[24,4,128]{2,1,0:T(4,128)S(1)} %get-tuple-element.18), channel_id=1, source_target_pairs={{2,0},{4,2},{6,4},{8,6},{10,8},{12,10},{14,12},{16,14},{18,16},{20... | collective-permute-start | bytes 147464 | tf_op jit(solution)/shard_map/ppermute | solution.py:24
  67.6 10.1 %collective-permute-start.12 = (f32[48,128]{1,0:T(8,128)S(1)}, f32[48,128]{1,0:T(8,128)S(1)}, u32[]{:S(2)}, u32[]{:S(2)}) collective-permute-start(f32[48,128]{1,0:T(8,128)S(1)} %pad_maximum_fusion.10), channel_id=1, source_target_pairs={{18,0},{20,2},{22,4},{24,6},{26,8},{28,10},{30,12},{0,14},{2,16},{... | collective-permute-start | bytes 73736 | tf_op jit(solution)/shard_map/ppermute | solution.py:24
  77.7 4.7 %collective-permute-start.13 = (f32[48,128]{1,0:T(8,128)S(1)}, f32[48,128]{1,0:T(8,128)S(1)}, u32[]{:S(2)}, u32[]{:S(2)}) collective-permute-start(f32[48,128]{1,0:T(8,128)S(1)} %pad_maximum_fusion.11), channel_id=1, source_target_pairs={{16,0},{18,2},{20,4},{22,6},{24,8},{26,10},{28,12},{30,14},{0,16},... | collective-permute-start | bytes 73736 | tf_op jit(solution)/shard_map/ppermute | solution.py:24
  82.5 5.6 %collective-permute-start.14 = (f32[48,128]{1,0:T(8,128)S(1)}, f32[48,128]{1,0:T(8,128)S(1)}, u32[]{:S(2)}, u32[]{:S(2)}) collective-permute-start(f32[48,128]{1,0:T(8,128)S(1)} %pad_maximum_fusion.12), channel_id=1, source_target_pairs={{14,0},{16,2},{18,4},{20,6},{22,8},{24,10},{26,12},{28,14},{30,16}... | collective-permute-start | bytes 73736 | tf_op jit(solution)/shard_map/ppermute | solution.py:24
  88.1 3.8 %collective-permute-start.15 = (f32[24,128]{1,0:T(8,128)S(1)}, f32[24,128]{1,0:T(8,128)S(1)}, u32[]{:S(2)}, u32[]{:S(2)}) collective-permute-start(f32[24,128]{1,0:T(8,128)S(1)} %get-tuple-element.26), channel_id=1, source_target_pairs={{2,0},{4,2},{6,4},{8,6},{10,8},{12,10},{14,12},{16,14},{18,16},{20... | collective-permute-start | bytes 36872 | tf_op jit(solution)/shard_map/ppermute | solution.py:24
  91.9 7.3 %collective-permute-start.16 = (f32[24,128]{1,0:T(8,128)S(1)}, f32[24,128]{1,0:T(8,128)S(1)}, u32[]{:S(2)}, u32[]{:S(2)}) collective-permute-start(f32[24,128]{1,0:T(8,128)S(1)} %get-tuple-element.25), channel_id=1, source_target_pairs={{30,0},{0,2},{2,4},{4,6},{6,8},{8,10},{10,12},{12,14},{14,16},{16,... | collective-permute-start | bytes 36872 | tf_op jit(solution)/shard_map/ppermute | solution.py:24
  99.1 7.7 %collective-permute-start.11 = (f32[24,4,128]{2,1,0:T(4,128)S(1)}, f32[24,4,128]{2,1,0:T(4,128)S(1)}, u32[]{:S(2)}, u32[]{:S(2)}) collective-permute-start(f32[24,4,128]{2,1,0:T(4,128)S(1)} %get-tuple-element.17), channel_id=1, source_target_pairs={{30,0},{0,2},{2,4},{4,6},{6,8},{8,10},{10,12},{12,14},{14,16},{16,... | collective-permute-start | bytes 147464 | tf_op jit(solution)/shard_map/ppermute | solution.py:24
  110.7 25.3 %copy-start.4 = (s32[64]{0:T(128)S(1)}, s32[64]{0:T(128)}, u32[]{:S(2)}) copy-start(s32[64]{0:T(128)} %param.15) | copy-start | bytes 772
  136.0 1.4 %collective-permute-start.17 = (f32[64,4,128]{2,0,1:T(8,128)S(1)}, f32[64,4,128]{2,0,1:T(8,128)S(1)}, u32[]{:S(2)}, u32[]{:S(2)}) collective-permute-start(f32[64,4,128]{2,0,1:T(8,128)S(1)} %copy.23), channel_id=1, source_target_pairs={{0,1},{1,0},{2,3},{3,2},{4,5},{5,4},{6,7},{7,6},{8,9},{9,8},{10,11... | collective-permute-start | bytes 393224 | tf_op jit(solution)/shard_map/ppermute | solution.py:47
